TPU v7x, 512 devices: a whole 4x4x16 slice. The times are simulated.
512 devices in a mesh: row: 32 (over z_lo, x), col: 16 (over y, z_hi, core).
Axes of the slice: x: 4, y: 4, z: 16 (z_hi: 2, z_lo: 8; z = z_hi * 8 + z_lo), core: 2. Of those that a mesh axis runs over, the one named last changes fastest.
Arguments:
- anc_inv: bfloat16 [16384, 16384], P('row', 'col'), may hold values from -0.0546875 to 0.0546875
- panel: bfloat16 [1, 12288, 2048], P(None, 'col', 'row'), may hold values from -6 to 6
- structure: int32 [1, 96], replicated, may hold values from 0 to 127, as said below
Outputs:
- off_inv: float32 [1, 16384, 2048], P(None, 'row', 'col')
Inputs may be any that keep to these rules, and one draw needn't show every extreme that they name: Each structure[s] holds 96 distinct ancestor block indices, in the order in which the panel stores its row blocks (not sorted); each group of 8 consecutive ancestor blocks holds 5 to 7 of them, and some group of each supernode holds exactly 7.
All inputs are finite; a program needn't handle non-finite values.
Results may differ from a plain program's by a relative error of at most 0.0003.
Values may be sent and summed in bfloat16 or wider, within the bound.
No kernel may reach another device: no remote copies, remote signals or barrier semaphores. Data moves between devices by JAX's collectives and lax.ppermute only.
A program may use at most 64 MiB of HBM per device.

v0:
```python
import jax
import jax.numpy as jnp
from jax import lax
from jax.sharding import PartitionSpec as P

BS = 128
SBLK = 96


def body(anc_inv, panel, structure):
    col_index = lax.axis_index("col")
    row_index = lax.axis_index("row")
    local_rows, local_cols = anc_inv.shape
    group_blocks = local_cols // BS
    local_width = panel.shape[2]
    gathered = lax.all_gather(panel, "col", axis=1, tiled=True)
    own_blocks = row_index * (local_rows // BS) + jnp.arange(local_rows // BS, dtype=jnp.int32)
    block_ids = jnp.arange(group_blocks, dtype=jnp.int32)
    blocks_of = structure[0]
    compact = gathered[0].reshape(SBLK, BS * local_width)
    local_block = blocks_of - col_index * group_blocks
    picker = (local_block[None, :] == block_ids[:, None]).astype(jnp.bfloat16)
    picked = (
        jnp.dot(picker, compact, preferred_element_type=jnp.float32)
        .astype(jnp.bfloat16)
        .reshape(group_blocks * BS, local_width)
    )
    partial_value = jnp.dot(
        anc_inv,
        lax.all_gather(picked, "row", axis=1, tiled=True),
        preferred_element_type=jnp.float32,
    )
    summed = lax.psum_scatter(partial_value, "col", scatter_dimension=1, tiled=True)
    member = jnp.any(blocks_of[None, :] == own_blocks[:, None], axis=1)
    row_mask = jnp.repeat(member, BS)
    results = [jnp.where(row_mask[:, None], -summed, jnp.zeros_like(summed))]
    return jnp.stack(results)


def solution(mesh):
    in_specs = (P("row", "col"), P(None, "col", "row"), P())
    out_specs = P(None, "row", "col")
    return jax.shard_map(body, mesh=mesh, in_specs=in_specs, out_specs=out_specs, check_vma=False)
```

profile of v0, /device:TPU:25, one launch (start us, length us, event | category | flops | bytes accessed | tf_op | source)
XLA Modules:
  0.0 493.6 jit_solution(13682171453870324515)
XLA Ops:
  6.5 0.0 copy-start
  6.5 0.0 all-gather.3.cloned.1.call-start
  6.5 0.7 all-gather.3.cloned.1.call-update
  7.3 0.0 all-gather.5.cloned.1.call-start
  7.3 0.7 subtract_bitcast_fusion
  8.0 91.9 %all-gather.3.cloned.1.call-done = bf16[1,12288,64]{1,2,0:T(8,128)(2,1)} async-done(((bf16[1,768,64]{1,2,0:T(8,128)(2,1)}), bf16[1,12288,64]{1,2,0:T(8,128)(2,1)}) %all-gather.3.cloned.1.call-update) | async-done | bytes 1572880 | tf_op jit(solution)/shard_map/all_gather | solution.py:16
  99.9 4.1 copy.10
  104.0 4.3 reshape_squeeze.3
  108.2 0.3 convolution_convert_fusion
  108.5 0.3 reshape.8
  108.8 0.8 copy.11
  109.6 0.0 all-gather.5.cloned.1.call-update
  109.6 0.0 reduce-scatter.2.cloned.1.call-start
  109.7 199.0 %all-gather.5.cloned.1.call-done = bf16[1024,2048]{0,1:T(8,128)(2,1)} async-done(((bf16[1024,64]{0,1:T(8,128)(2,1)}), bf16[1024,2048]{0,1:T(8,128)(2,1)}) %all-gather.5.cloned.1.call-update) | async-done | bytes 4194320 | tf_op jit(solution)/shard_map/all_gather | solution.py:30
  308.7 0.0 copy-done
  308.7 6.5 %convolution_bitcast_fusion = f32[512,2048]{0,1:T(8,128)} fusion(bf16[1024,2048]{0,1:T(8,128)(2,1)} %all-gather.5.cloned.1.call-done, bf16[512,1024]{1,0:T(8,128)(2,1)S(1)} %copy-done), kind=kOutput, calls=%fused_computation.1 | convolution fusion | flops 2147483648 | bytes 9437184 | tf_op jit(solution)/shard_map/dot_general | solution.py:28
  315.2 0.0 copy-start.1
  315.2 0.0 reduce-scatter.2.cloned.1.call-update
  315.3 0.6 copy-done.1
  315.9 0.2 compare_reduce_fusion
  316.1 0.1 broadcast_bitcast_fusion
  316.1 169.1 %reduce-scatter.2.cloned.1.call-done = f32[512,128]{0,1:T(8,128)} async-done(((f32[512,2048]{0,1:T(8,128)}), f32[512,128]{0,1:T(8,128)}) %reduce-scatter.2.cloned.1.call-update) | async-done | bytes 262160 | tf_op jit(solution)/shard_map/reduce_scatter | solution.py:33
  485.2 1.0 select_bitcast_fusion
  486.2 0.8 copy.12
  (1 shorter events, 0.0 us)
Async XLA Ops:
  6.5 302.2 %copy-start = (bf16[512,1024]{1,0:T(8,128)(2,1)S(1)}, bf16[512,1024]{1,0:T(8,128)(2,1)}, u32[]{:S(2)}) copy-start(bf16[512,1024]{1,0:T(8,128)(2,1)} %param.3) | copy-start | bytes 3145732
  6.5 93.3 %all-gather.3.cloned.1.call-start = ((), (), s32[]{:S(2)}) async-start(), calls=%async_computation.1 | async-start | bytes 1671168 | tf_op jit(solution)/shard_map/all_gather | solution.py:16
  7.3 301.5 %all-gather.5.cloned.1.call-start = ((), (), s32[]{:S(2)}) async-start(), calls=%async_computation.2 | async-start | bytes 4325376 | tf_op jit(solution)/shard_map/all_gather | solution.py:30
  109.6 375.6 %reduce-scatter.2.cloned.1.call-start = ((), (), s32[]{:S(2)}) async-start(), calls=%async_computation.3 | async-start | bytes 4456448 | tf_op jit(solution)/shard_map/reduce_scatter | solution.py:33
  315.2 0.7 copy-start.1
Sparse Core Ops, SparseCore 0:
  10.6 89.1 all-gather.2
  109.7 198.9 all-gather.4
  315.4 169.8 reduce-scatter.1
where the time goes:
time: 496 us; the launch traced here: 494 us
  waiting for transfers between devices  461 us (93%)
  between operations  13.2 us (3%)
  local copies, waits for them, and re-layouts  11 us (2%)
  matrix products  6.81 us (1%)
    all_gather x1, waiting for transfers between devices, body(): lax.all_gather(picked, 'row', axis=1, tiled=True)  199 us
    reduce_scatter x1, waiting for transfers between devices, body(): lax.psum_scatter(partial_value, 'col', scatter_dimension=1, tiled=True)  169 us
    all_gather x1, waiting for transfers between devices, body(): gathered = lax.all_gather(panel, 'col', axis=1, tiled=True)  91.9 us
  transfers between devices with their start and end apart: 3, of which 3 were waited for; matrix products, arithmetic and copies ran while one was open for 0% of the time, Pallas kernels for 0%

commit v1 on v0

v1 whole, which is shorter than its diff:
```python
import jax
import jax.numpy as jnp
from jax import lax
from jax.sharding import Mesh, PartitionSpec as P

BS = 128
SBLK = 96
ROW = ("zl", "x")
COL = ("y", "zh", "c")


def body(anc_inv, panel, structure):
    col_index = lax.axis_index(COL)
    row_index = lax.axis_index(ROW)
    local_rows, local_cols = anc_inv.shape
    group_blocks = local_cols // BS
    local_width = panel.shape[2]
    gathered = lax.all_gather(panel, COL, axis=1, tiled=True)
    own_blocks = row_index * (local_rows // BS) + jnp.arange(local_rows // BS, dtype=jnp.int32)
    block_ids = jnp.arange(group_blocks, dtype=jnp.int32)
    blocks_of = structure[0]
    compact = gathered[0].reshape(SBLK, BS * local_width)
    local_block = blocks_of - col_index * group_blocks
    picker = (local_block[None, :] == block_ids[:, None]).astype(jnp.bfloat16)
    picked = (
        jnp.dot(picker, compact, preferred_element_type=jnp.float32)
        .astype(jnp.bfloat16)
        .reshape(group_blocks * BS, local_width)
    )
    partial_value = jnp.dot(
        anc_inv,
        lax.all_gather(lax.all_gather(picked, "x", axis=1, tiled=True), "zl", axis=1, tiled=True),
        preferred_element_type=jnp.float32,
    )
    summed = lax.psum_scatter(partial_value, COL, scatter_dimension=1, tiled=True)
    member = jnp.any(blocks_of[None, :] == own_blocks[:, None], axis=1)
    row_mask = jnp.repeat(member, BS)
    results = [jnp.where(row_mask[:, None], -summed, jnp.zeros_like(summed))]
    return jnp.stack(results)


def solution(mesh):
    rows, cols = mesh.shape["row"], mesh.shape["col"]
    fine = Mesh(mesh.devices.reshape(rows // 4, 4, cols // 4, 2, 2), ("zl", "x", "y", "zh", "c"))
    in_specs = (P(ROW, COL), P(None, COL, ROW), P())
    out_specs = P(None, ROW, COL)
    return jax.shard_map(body, mesh=fine, in_specs=in_specs, out_specs=out_specs, check_vma=False)
```

time: 496 us -> 382 us (0.77)
  waiting for transfers between devices: 461 us -> 336 us
  blocking collectives: 0 us -> 11.2 us
    all_gather x2, waiting for transfers between devices: 291 us -> 189 us  [the longest x1 97.4 us: body(): lax.all_gather(lax.all_gather(picked, 'x', axis=1, tiled=True), 'zl', axi...]
    reduce_scatter x1, waiting for transfers between devices: 169 us -> 146 us  [body(): lax.psum_scatter(partial_value, COL, scatter_dimension=1, tiled=True)]
    all_gather x0 -> x1, blocking collectives: none -> 11.2 us  [body(): lax.all_gather(picked, 'x', axis=1, tiled=True)]
where the time goes in v1:
time: 382 us; the launch traced here: 379 us
  waiting for transfers between devices  336 us (88%)
  between operations  13.2 us (3%)
  blocking collectives  11.2 us (3%)
  local copies, waits for them, and re-layouts  10.3 us (3%)
  matrix products  6.85 us (2%)
    reduce_scatter x1, waiting for transfers between devices, body(): lax.psum_scatter(partial_value, COL, scatter_dimension=1, tiled=True)  146 us
    all_gather x1, waiting for transfers between devices, body(): lax.all_gather(lax.all_gather(picked, 'x', axis=1, tiled=True), 'zl', axi...  97.4 us
    all_gather x1, waiting for transfers between devices, body(): gathered = lax.all_gather(panel, COL, axis=1, tiled=True)  91.9 us
    all_gather x1, blocking collectives, body(): lax.all_gather(picked, 'x', axis=1, tiled=True)  11.2 us
  transfers between devices with their start and end apart: 3, of which 3 were waited for; matrix products, arithmetic and copies ran while one was open for 0% of the time, Pallas kernels for 0%

profile of v1, /device:TPU:25, one launch (start us, length us, event | category | flops | bytes accessed | tf_op | source)
XLA Modules:
  0.0 379.2 jit_solution(18023949575931893657)
XLA Ops:
  6.5 0.0 copy-start
  6.5 0.0 all-gather.3.cloned.1.call-start
  6.5 0.7 all-gather.3.cloned.1.call-update
  7.3 0.0 all-gather.5.cloned.1.call-start
  7.3 0.7 subtract_bitcast_fusion
  8.0 91.9 %all-gather.3.cloned.1.call-done = bf16[1,12288,64]{1,2,0:T(8,128)(2,1)} async-done(((bf16[1,768,64]{1,2,0:T(8,128)(2,1)}), bf16[1,12288,64]{1,2,0:T(8,128)(2,1)}) %all-gather.3.cloned.1.call-update) | async-done | bytes 1572880 | tf_op jit(solution)/shard_map/all_gather | solution.py:18
  99.9 4.1 %copy.10 = bf16[1,12288,64]{2,1,0:T(8,128)(2,1)} copy(bf16[1,12288,64]{1,2,0:T(8,128)(2,1)} %all-gather.3.cloned.1.call-done) | data formatting | bytes 3145728 | tf_op jit(solution)/shard_map/all_gather | solution.py:18
  104.0 4.3 %reshape_squeeze.3 = bf16[96,8192]{1,0:T(8,128)(2,1)S(1)} reshape(bf16[1,12288,64]{2,1,0:T(8,128)(2,1)} %copy.10) | data formatting | bytes 3145728 | tf_op jit(solution)/shard_map/reshape;squeeze | solution.py:22
  108.2 0.3 convolution_convert_fusion
  108.5 0.3 reshape.8
  108.8 0.1 copy.11
  109.0 11.2 %all_gather.10 = bf16[1024,256]{0,1:T(8,128)(2,1)} all-gather(bf16[1024,64]{0,1:T(8,128)(2,1)S(1)} %copy.11), channel_id=1, replica_groups=mesh['zl'=8,'x'=4,'y'=4,'zh'=2,'c'=2] {'x'}, dimensions={1}, use_global_device_ids=true | all-gather | bytes 655360 | tf_op jit(solution)/shard_map/all_gather | solution.py:32
  120.2 0.0 all-gather.5.cloned.1.call-update
  120.2 0.0 reduce-scatter.2.cloned.1.call-start
  120.3 97.4 %all-gather.5.cloned.1.call-done = bf16[1024,2048]{0,1:T(8,128)(2,1)} async-done(((bf16[1024,256]{0,1:T(8,128)(2,1)}), bf16[1024,2048]{0,1:T(8,128)(2,1)}) %all-gather.5.cloned.1.call-update) | async-done | bytes 4194320 | tf_op jit(solution)/shard_map/all_gather | solution.py:32
  217.7 0.0 copy-done
  217.7 6.5 %convolution_bitcast_fusion = f32[512,2048]{0,1:T(8,128)} fusion(bf16[1024,2048]{0,1:T(8,128)(2,1)} %all-gather.5.cloned.1.call-done, bf16[512,1024]{1,0:T(8,128)(2,1)S(1)} %copy-done), kind=kOutput, calls=%fused_computation.1 | convolution fusion | flops 2147483648 | bytes 9437184 | tf_op jit(solution)/shard_map/dot_general | solution.py:30
  224.2 0.0 copy-start.1
  224.3 0.0 reduce-scatter.2.cloned.1.call-update
  224.3 0.6 copy-done.1
  224.9 0.2 compare_reduce_fusion
  225.1 0.1 broadcast_bitcast_fusion
  225.2 145.7 %reduce-scatter.2.cloned.1.call-done = f32[512,128]{0,1:T(8,128)} async-done(((f32[512,2048]{0,1:T(8,128)}), f32[512,128]{0,1:T(8,128)}) %reduce-scatter.2.cloned.1.call-update) | async-done | bytes 262160 | tf_op jit(solution)/shard_map/reduce_scatter | solution.py:35
  370.8 1.0 select_bitcast_fusion
  371.8 0.8 copy.12
  (1 shorter events, 0.0 us)
Async XLA Ops:
  6.5 211.2 %copy-start = (bf16[512,1024]{1,0:T(8,128)(2,1)S(1)}, bf16[512,1024]{1,0:T(8,128)(2,1)}, u32[]{:S(2)}) copy-start(bf16[512,1024]{1,0:T(8,128)(2,1)} %param.3) | copy-start | bytes 3145732
  6.5 93.3 %all-gather.3.cloned.1.call-start = ((), (), s32[]{:S(2)}) async-start(), calls=%async_computation.1 | async-start | bytes 1671168 | tf_op jit(solution)/shard_map/all_gather | solution.py:18
  7.3 210.4 %all-gather.5.cloned.1.call-start = ((), (), s32[]{:S(2)}) async-start(), calls=%async_computation.2 | async-start | bytes 4718592 | tf_op jit(solution)/shard_map/all_gather | solution.py:32
  120.2 250.6 %reduce-scatter.2.cloned.1.call-start = ((), (), s32[]{:S(2)}) async-start(), calls=%async_computation.3 | async-start | bytes 4456448 | tf_op jit(solution)/shard_map/reduce_scatter | solution.py:35
  224.2 0.7 copy-start.1
Sparse Core Ops, SparseCore 0:
  10.6 89.1 all-gather.2
  120.3 97.3 all-gather.4
  224.4 146.4 reduce-scatter.1

commit v2 on v1

v2 whole, which is shorter than its diff:
```python
import jax
import jax.numpy as jnp
from jax import lax
from jax.sharding import Mesh, PartitionSpec as P

BS = 128
SBLK = 96
ROW = ("zl", "x")
COL = ("y", "zh", "c")


def body(anc_inv, panel, structure):
    n_y, n_zh, n_c = lax.axis_size("y"), lax.axis_size("zh"), lax.axis_size("c")
    col_index = lax.axis_index(COL)
    row_index = lax.axis_index(ROW)
    zh_index = lax.axis_index("zh")
    local_rows, local_cols = anc_inv.shape
    group_blocks = local_cols // BS
    local_width = panel.shape[2]
    per_dev = panel.shape[1] // BS
    gathered = lax.all_gather(panel[0], "zh", axis=0, tiled=True)
    gathered = lax.all_gather(gathered, ("y", "c"), axis=0, tiled=True)
    blocks_of = structure[0]
    blocks_gathered = blocks_of.reshape(n_y, n_zh, n_c, per_dev).transpose(0, 2, 1, 3).reshape(SBLK)
    own_blocks = row_index * (local_rows // BS) + jnp.arange(local_rows // BS, dtype=jnp.int32)
    block_ids = jnp.arange(group_blocks, dtype=jnp.int32)
    compact = gathered.reshape(SBLK, BS * local_width)
    local_block = blocks_gathered - col_index * group_blocks
    picker = (local_block[None, :] == block_ids[:, None]).astype(jnp.bfloat16)
    picked = (
        jnp.dot(picker, compact, preferred_element_type=jnp.float32)
        .astype(jnp.bfloat16)
        .reshape(group_blocks * BS, local_width)
    )
    expanded = lax.all_gather(lax.all_gather(picked, "x", axis=1, tiled=True), "zl", axis=1, tiled=True)
    width = expanded.shape[1]
    chunk = width // (n_y * n_zh * n_c)
    rhs = expanded.reshape(-1, n_y, n_zh, n_c, chunk)
    partial_value = jnp.einsum("mk,kyzcn->yczmn", anc_inv, rhs, preferred_element_type=jnp.float32)
    partial_value = partial_value.reshape(n_y * n_c, n_zh, local_rows, chunk)
    halves = lax.psum_scatter(partial_value, ("y", "c"), scatter_dimension=0, tiled=True)[0]
    mine = lax.dynamic_index_in_dim(halves, zh_index, 0, keepdims=False)
    other = lax.dynamic_index_in_dim(halves, 1 - zh_index, 0, keepdims=False)
    summed = mine + lax.ppermute(other, "zh", [(0, 1), (1, 0)])
    member = jnp.any(blocks_of[None, :] == own_blocks[:, None], axis=1)
    row_mask = jnp.repeat(member, BS)
    results = [jnp.where(row_mask[:, None], -summed, jnp.zeros_like(summed))]
    return jnp.stack(results)


def solution(mesh):
    rows, cols = mesh.shape["row"], mesh.shape["col"]
    fine = Mesh(mesh.devices.reshape(rows // 4, 4, cols // 4, 2, 2), ("zl", "x", "y", "zh", "c"))
    in_specs = (P(ROW, COL), P(None, COL, ROW), P())
    out_specs = P(None, ROW, COL)
    return jax.shard_map(body, mesh=fine, in_specs=in_specs, out_specs=out_specs, check_vma=False)
```

time: 382 us -> 283 us (0.74)
  waiting for transfers between devices: 336 us -> 203 us
  blocking collectives: 11.2 us -> 29.8 us
  starting transfers between devices: 0.08 us -> 11.9 us
  local copies, waits for them, and re-layouts: 10.3 us -> 15.3 us
    reduce_scatter x1, waiting for transfers between devices: 146 us -> 39.4 us  [body(): lax.psum_scatter(partial_value, ('y', 'c'), scatter_dimension=0, tiled=True)]
    all_gather x1, waiting for transfers between devices: 91.9 us -> 33.9 us  [body(): gathered = lax.all_gather(gathered, ('y', 'c'), axis=0, tiled=True)]
    ppermute x0 -> x1, waiting for transfers between devices: none -> 21.6 us  [body(): summed = mine + lax.ppermute(other, 'zh', [(0, 1), (1, 0)])]
    all_gather x0 -> x1, blocking collectives: none -> 18.7 us  [body(): gathered = lax.all_gather(panel[0], 'zh', axis=0, tiled=True)]
    ppermute x0 -> x1, starting transfers between devices: none -> 11.8 us  [body(): summed = mine + lax.ppermute(other, 'zh', [(0, 1), (1, 0)])]
    all_gather x1, waiting for transfers between devices: 97.4 us -> 108 us  [body(): lax.all_gather(lax.all_gather(picked, 'x', axis=1, tiled=True), 'zl', axi...]
    transpose x0 -> x1, local copies, waits for them, and re-layouts: none -> 5.23 us  [body(): jnp.einsum('mk,kyzcn->yczmn', anc_inv, rhs, preferred_element_type=jnp.fl...]
    another operation x2 -> x0, local copies, waits for them, and re-layouts: 5.09 us -> none  [the longest x1 4.26 us: body(): compact = gathered[0].reshape(SBLK, BS * local_width)]
  transfers between devices with their start and end apart: 3 -> 4, of which waited for: 3 -> 4; matrix products, arithmetic and copies ran while one was open for 0% -> 0% of each run, Pallas kernels for 0% -> 0%
where the time goes in v2:
time: 283 us
  waiting for transfers between devices  203 us (72%)
  blocking collectives  29.8 us (11%)
  local copies, waits for them, and re-layouts  15.3 us (5%)
  between operations  13.2 us (5%)
  starting transfers between devices  11.9 us (4%)
  matrix products  6.85 us (2%)
    all_gather x1, waiting for transfers between devices, body(): lax.all_gather(lax.all_gather(picked, 'x', axis=1, tiled=True), 'zl', axi...  108 us
    reduce_scatter x1, waiting for transfers between devices, body(): lax.psum_scatter(partial_value, ('y', 'c'), scatter_dimension=0, tiled=True)  39.4 us
    all_gather x1, waiting for transfers between devices, body(): gathered = lax.all_gather(gathered, ('y', 'c'), axis=0, tiled=True)  33.9 us
    ppermute x1, waiting for transfers between devices, body(): summed = mine + lax.ppermute(other, 'zh', [(0, 1), (1, 0)])  21.6 us
    all_gather x1, blocking collectives, body(): gathered = lax.all_gather(panel[0], 'zh', axis=0, tiled=True)  18.7 us
    ppermute x1, starting transfers between devices, body(): summed = mine + lax.ppermute(other, 'zh', [(0, 1), (1, 0)])  11.8 us
    all_gather x1, blocking collectives, body(): lax.all_gather(picked, 'x', axis=1, tiled=True)  11.2 us
    dot_general x1, matrix products, body(): jnp.einsum('mk,kyzcn->yczmn', anc_inv, rhs, preferred_element_type=jnp.fl...  6.54 us
  transfers between devices with their start and end apart: 4, of which 4 were waited for; matrix products, arithmetic and copies ran while one was open for 0% of the time, Pallas kernels for 0%

profile of v2, /device:TPU:25, one launch (start us, length us, event | category | flops | bytes accessed | tf_op | source)
XLA Modules:
  0.0 282.7 jit_solution(7589429934079507593)
XLA Ops:
  6.5 0.0 copy-start
  6.5 0.0 all-gather.7.cloned.1.call-start
  6.5 18.7 %all-gather = bf16[1,1536,64]{1,2,0:T(8,128)(2,1)} all-gather(bf16[1,768,64]{1,2,0:T(8,128)(2,1)} %param.4), channel_id=2, replica_groups=mesh['zl'=8,'x'=4,'y'=4,'zh'=2,'c'=2] {'zh'}, dimensions={1}, use_global_device_ids=true | all-gather | bytes 294912 | tf_op jit(solution)/shard_map/all_gather | solution.py:21
  25.2 0.0 all-gather.7.cloned.1.call-update
  25.2 0.0 all-gather.5.cloned.1.call-start
  25.3 0.7 subtract_reduce_fusion
  26.0 0.1 sub.24
  26.1 0.1 sub.26
  26.2 33.9 %all-gather.7.cloned.1.call-done = bf16[1,12288,64]{1,2,0:T(8,128)(2,1)} async-done(((bf16[1,1536,64]{1,2,0:T(8,128)(2,1)}), bf16[1,12288,64]{1,2,0:T(8,128)(2,1)}) %all-gather.7.cloned.1.call-update) | async-done | bytes 1572880 | tf_op jit(solution)/shard_map/all_gather | solution.py:22
  60.1 4.1 %copy.15 = bf16[1,12288,64]{2,1,0:T(8,128)(2,1)} copy(bf16[1,12288,64]{1,2,0:T(8,128)(2,1)} %all-gather.7.cloned.1.call-done) | data formatting | bytes 3145728 | tf_op jit(solution)/shard_map/all_gather | solution.py:22
  64.3 4.3 %reshape.31 = bf16[96,8192]{1,0:T(8,128)(2,1)S(1)} reshape(bf16[1,12288,64]{2,1,0:T(8,128)(2,1)} %copy.15) | data formatting | bytes 3145728 | tf_op jit(solution)/shard_map/reshape | solution.py:27
  68.5 0.3 convolution_convert_fusion
  68.8 0.3 reshape.32
  69.1 0.1 copy.16
  69.2 11.2 %all_gather.14 = bf16[1024,256]{0,1:T(8,128)(2,1)} all-gather(bf16[1024,64]{0,1:T(8,128)(2,1)S(1)} %copy.16), channel_id=1, replica_groups=mesh['zl'=8,'x'=4,'y'=4,'zh'=2,'c'=2] {'x'}, dimensions={1}, use_global_device_ids=true | all-gather | bytes 655360 | tf_op jit(solution)/shard_map/all_gather | solution.py:35
  80.4 0.0 all-gather.5.cloned.1.call-update
  80.4 0.0 reduce-scatter.2.cloned.1.call-start
  80.5 108.0 %all-gather.5.cloned.1.call-done = bf16[1024,2048]{0,1:T(8,128)(2,1)} async-done(((bf16[1024,256]{0,1:T(8,128)(2,1)}), bf16[1024,2048]{0,1:T(8,128)(2,1)}) %all-gather.5.cloned.1.call-update) | async-done | bytes 4194320 | tf_op jit(solution)/shard_map/all_gather | solution.py:35
  188.5 0.0 copy-done
  188.5 6.5 %convolution_bitcast_fusion = f32[4,2,2,512,128]{3,4,1,2,0:T(8,128)} fusion(bf16[1024,4,2,2,128]{0,4,3,2,1:T(8,128)(2,1)} %bitcast.29, bf16[512,1024]{1,0:T(8,128)(2,1)S(1)} %copy-done), kind=kOutput, calls=%fused_computation.1 | convolution fusion | flops 2147483648 | bytes 9437184 | tf_op jit(solution)/shard_map/mk,kyzcn->yczmn/dot_general | solution.py:39
  195.1 5.2 %copy.17 = f32[4,2,2,512,128]{4,3,2,1,0:T(8,128)} copy(f32[4,2,2,512,128]{3,4,1,2,0:T(8,128)} %convolution_bitcast_fusion) | data formatting | bytes 8388608 | tf_op jit(solution)/shard_map/mk,kyzcn->yczmn/transpose | solution.py:39
  200.3 0.0 copy-start.1
  200.3 0.0 reduce-scatter.2.cloned.1.call-update
  200.3 39.4 %reduce-scatter.2.cloned.1.call-done = f32[1,2,512,128]{3,2,1,0:T(8,128)} async-done(((f32[8,2,512,128]{3,2,1,0:T(8,128)}), f32[1,2,512,128]{3,2,1,0:T(8,128)}) %reduce-scatter.2.cloned.1.call-update) | async-done | bytes 524304 | tf_op jit(solution)/shard_map/reduce_scatter | solution.py:41
  239.7 1.0 dynamic-slice_bitcast_fusion
  240.7 11.8 %collective-permute-start = (f32[512,128]{1,0:T(8,128)S(1)}, f32[512,128]{1,0:T(8,128)S(1)}, u32[]{:S(2)}, u32[]{:S(2)}) collective-permute-start(f32[512,128]{1,0:T(8,128)S(1)} %dynamic-slice_bitcast_fusion), channel_id=1, source_target_pairs={{0,2},{2,0},{1,3},{3,1},{4,6},{6,4},{5,7},{7,5},{8,10},{10,8},{9,1... | collective-permute-start | bytes 786440 | tf_op jit(solution)/shard_map/ppermute | solution.py:44
  252.5 0.0 copy-done.1
  252.5 0.2 compare_reduce_fusion
  252.7 0.1 broadcast_bitcast_fusion
  252.7 21.6 %collective-permute-done = f32[512,128]{1,0:T(8,128)S(1)} collective-permute-done((f32[512,128]{1,0:T(8,128)S(1)}, f32[512,128]{1,0:T(8,128)S(1)}, u32[]{:S(2)}, u32[]{:S(2)}) %collective-permute-start) | collective-permute-done | bytes 262176 | tf_op jit(solution)/shard_map/ppermute | solution.py:44
  274.4 1.8 fusion.3
  (2 shorter events, 0.0 us)
Async XLA Ops:
  6.5 182.0 %copy-start = (bf16[512,1024]{1,0:T(8,128)(2,1)S(1)}, bf16[512,1024]{1,0:T(8,128)(2,1)}, u32[]{:S(2)}) copy-start(bf16[512,1024]{1,0:T(8,128)(2,1)} %param.3) | copy-start | bytes 3145732
  6.5 53.6 %all-gather.7.cloned.1.call-start = ((), (), s32[]{:S(2)}) async-start(), calls=%async_computation.3 | async-start | bytes 1769472 | tf_op jit(solution)/shard_map/all_gather | solution.py:22
  25.2 163.3 %all-gather.5.cloned.1.call-start = ((), (), s32[]{:S(2)}) async-start(), calls=%async_computation.1 | async-start | bytes 4718592 | tf_op jit(solution)/shard_map/all_gather | solution.py:35
  80.4 159.3 %reduce-scatter.2.cloned.1.call-start = ((), (), s32[]{:S(2)}) async-start(), calls=%async_computation.2 | async-start | bytes 4718592 | tf_op jit(solution)/shard_map/reduce_scatter | solution.py:41
  200.3 52.2 %copy-start.1 = (s32[1,96]{1,0:T(1,128)S(1)}, s32[1,96]{1,0:T(1,128)}, u32[]{:S(2)}) copy-start(s32[1,96]{1,0:T(1,128)} %param.5) | copy-start | bytes 1156
  240.7 33.7 %collective-permute-start = (f32[512,128]{1,0:T(8,128)S(1)}, f32[512,128]{1,0:T(8,128)S(1)}, u32[]{:S(2)}, u32[]{:S(2)}) collective-permute-start(f32[512,128]{1,0:T(8,128)S(1)} %dynamic-slice_bitcast_fusion), channel_id=1, source_target_pairs={{0,2},{2,0},{1,3},{3,1},{4,6},{6,4},{5,7},{7,5},{8,10},{10,8},{9,1... | collective-permute-start | bytes 786440 | tf_op jit(solution)/shard_map/ppermute | solution.py:44
Sparse Core Ops, SparseCore 0:
  25.4 34.7 all-gather.6
  80.5 107.9 all-gather.4
  200.4 39.2 reduce-scatter.1

commit v3 on v2

--- a/solution.py
+++ b/solution.py
@@ -5,6 +5,7 @@
 
 BS = 128
 SBLK = 96
+CAP = 7
 ROW = ("zl", "x")
 COL = ("y", "zh", "c")
 
@@ -26,17 +27,24 @@
     block_ids = jnp.arange(group_blocks, dtype=jnp.int32)
     compact = gathered.reshape(SBLK, BS * local_width)
     local_block = blocks_gathered - col_index * group_blocks
-    picker = (local_block[None, :] == block_ids[:, None]).astype(jnp.bfloat16)
+    hits = local_block[None, :] == block_ids[:, None]
+    present = jnp.any(hits, axis=1)
+    rank = jnp.cumsum(present.astype(jnp.int32)) - 1
+    slot_ids = jnp.arange(CAP, dtype=jnp.int32)
+    slot_of = present[None, :] & (rank[None, :] == slot_ids[:, None])
+    picker = jnp.dot(slot_of.astype(jnp.float32), hits.astype(jnp.float32)).astype(jnp.bfloat16)
+    slot_block = jnp.sum(jnp.where(slot_of, block_ids[None, :], 0), axis=1)
     picked = (
         jnp.dot(picker, compact, preferred_element_type=jnp.float32)
         .astype(jnp.bfloat16)
-        .reshape(group_blocks * BS, local_width)
+        .reshape(CAP * BS, local_width)
     )
+    anc_kept = jnp.take(anc_inv.reshape(local_rows, group_blocks, BS), slot_block, axis=1).reshape(local_rows, CAP * BS)
     expanded = lax.all_gather(lax.all_gather(picked, "x", axis=1, tiled=True), "zl", axis=1, tiled=True)
     width = expanded.shape[1]
     chunk = width // (n_y * n_zh * n_c)
     rhs = expanded.reshape(-1, n_y, n_zh, n_c, chunk)
-    partial_value = jnp.einsum("mk,kyzcn->yczmn", anc_inv, rhs, preferred_element_type=jnp.float32)
+    partial_value = jnp.einsum("mk,kyzcn->yczmn", anc_kept, rhs, preferred_element_type=jnp.float32)
     partial_value = partial_value.reshape(n_y * n_c, n_zh, local_rows, chunk)
     halves = lax.psum_scatter(partial_value, ("y", "c"), scatter_dimension=0, tiled=True)[0]
     mine = lax.dynamic_index_in_dim(halves, zh_index, 0, keepdims=False)

time: 283 us -> 272 us (0.961)
  waiting for transfers between devices: 203 us -> 189 us
    all_gather x1, waiting for transfers between devices: 108 us -> 94.6 us  [body(): lax.all_gather(lax.all_gather(picked, 'x', axis=1, tiled=True), 'zl', axi...]
  transfers between devices with their start and end apart: 4 -> 4, of which waited for: 4 -> 4; matrix products, arithmetic and copies ran while one was open for 0% -> 2% of each run, Pallas kernels for 0% -> 0%
where the time goes in v3:
time: 272 us; the launch traced here: 271 us
  waiting for transfers between devices  189 us (69%)
  blocking collectives  29.5 us (11%)
  local copies, waits for them, and re-layouts  15.8 us (6%)
  between operations  13.2 us (5%)
  starting transfers between devices  11.9 us (4%)
  matrix products  8.21 us (3%)
  other arithmetic  3.26 us (1%)
    all_gather x1, waiting for transfers between devices, body(): lax.all_gather(lax.all_gather(picked, 'x', axis=1, tiled=True), 'zl', axi...  94.6 us
    reduce_scatter x1, waiting for transfers between devices, body(): lax.psum_scatter(partial_value, ('y', 'c'), scatter_dimension=0, tiled=True)  39.2 us
    all_gather x1, waiting for transfers between devices, body(): gathered = lax.all_gather(gathered, ('y', 'c'), axis=0, tiled=True)  33.6 us
    ppermute x1, waiting for transfers between devices, body(): summed = mine + lax.ppermute(other, 'zh', [(0, 1), (1, 0)])  21.7 us
    all_gather x1, blocking collectives, body(): gathered = lax.all_gather(panel[0], 'zh', axis=0, tiled=True)  18.5 us
    ppermute x1, starting transfers between devices, body(): summed = mine + lax.ppermute(other, 'zh', [(0, 1), (1, 0)])  11.8 us
    all_gather x1, blocking collectives, body(): lax.all_gather(picked, 'x', axis=1, tiled=True)  11 us
    dot_general x1, matrix products, body(): jnp.einsum('mk,kyzcn->yczmn', anc_kept, rhs, preferred_element_type=jnp.f...  6.3 us
  transfers between devices with their start and end apart: 4, of which 4 were waited for; matrix products, arithmetic and copies ran while one was open for 2% of the time, Pallas kernels for 0%

profile of v3, /device:TPU:25, one launch (start us, length us, event | category | flops | bytes accessed | tf_op | source)
XLA Modules:
  0.0 271.1 jit_solution(8857181893159621699)
XLA Ops:
  6.5 0.0 all-gather.7.cloned.1.call-start
  6.5 18.5 %all-gather = bf16[1,1536,64]{1,2,0:T(8,128)(2,1)} all-gather(bf16[1,768,64]{1,2,0:T(8,128)(2,1)} %param.4), channel_id=2, replica_groups=mesh['zl'=8,'x'=4,'y'=4,'zh'=2,'c'=2] {'zh'}, dimensions={1}, use_global_device_ids=true | all-gather | bytes 294912 | tf_op jit(solution)/shard_map/all_gather | solution.py:22
  25.1 0.0 all-gather.7.cloned.1.call-update
  25.1 0.0 all-gather.5.cloned.1.call-start
  25.2 0.7 subtract_reduce_fusion
  25.8 0.1 sub.29
  25.9 0.1 sub.31
  26.0 0.1 fusion.3
  26.2 0.2 reduce-window.8
  26.4 33.6 %all-gather.7.cloned.1.call-done = bf16[1,12288,64]{1,2,0:T(8,128)(2,1)} async-done(((bf16[1,1536,64]{1,2,0:T(8,128)(2,1)}), bf16[1,12288,64]{1,2,0:T(8,128)(2,1)}) %all-gather.7.cloned.1.call-update) | async-done | bytes 1572880 | tf_op jit(solution)/shard_map/all_gather | solution.py:23
  60.0 3.1 %copy.29 = bf16[1,12288,64]{2,1,0:T(8,128)(2,1)S(1)} copy(bf16[1,12288,64]{1,2,0:T(8,128)(2,1)} %all-gather.7.cloned.1.call-done) | data formatting | bytes 3145728 | tf_op jit(solution)/shard_map/all_gather | solution.py:23
  63.1 3.5 %reshape.118 = bf16[96,8192]{1,0:T(8,128)(2,1)} reshape(bf16[1,12288,64]{2,1,0:T(8,128)(2,1)S(1)} %copy.29) | data formatting | bytes 3145728 | tf_op jit(solution)/shard_map/reshape | solution.py:28
  66.5 0.0 copy-start
  66.5 1.9 convolution_convert_fusion
  68.4 0.2 reshape.119
  68.7 0.1 copy.30
  68.8 11.0 %all_gather.14 = bf16[896,256]{0,1:T(8,128)(2,1)} all-gather(bf16[896,64]{0,1:T(8,128)(2,1)S(1)} %copy.30), channel_id=1, replica_groups=mesh['zl'=8,'x'=4,'y'=4,'zh'=2,'c'=2] {'x'}, dimensions={1}, use_global_device_ids=true | all-gather | bytes 573440 | tf_op jit(solution)/shard_map/all_gather | solution.py:43
  79.8 0.0 all-gather.5.cloned.1.call-update
  79.8 0.0 reduce-scatter.2.cloned.1.call-start
  79.8 0.0 copy-done
  79.9 0.5 copy.31
  80.4 0.7 copy.32
  81.1 0.1 select_reduce_fusion
  81.2 0.7 gather_fusion
  82.0 0.2 select_bitcast_fusion
  82.1 0.5 copy.33
  82.6 94.6 %all-gather.5.cloned.1.call-done = bf16[896,2048]{0,1:T(8,128)(2,1)} async-done(((bf16[896,256]{0,1:T(8,128)(2,1)}), bf16[896,2048]{0,1:T(8,128)(2,1)}) %all-gather.5.cloned.1.call-update) | async-done | bytes 3670032 | tf_op jit(solution)/shard_map/all_gather | solution.py:43
  177.3 6.3 %convolution_bitcast_fusion = f32[4,2,2,512,128]{3,4,1,2,0:T(8,128)} fusion(bf16[896,4,2,2,128]{0,4,3,2,1:T(8,128)(2,1)} %bitcast.41, bf16[512,896,1,1,1]{0,1,4,3,2:T(8,128)(2,1)S(1)} %bitcast.39), kind=kOutput, calls=%fused_computation.2 | convolution fusion | flops 1879048192 | bytes 8781824 | tf_op jit(solution)/shard_map/mk,kyzcn->yczmn/dot_general | solution.py:47
  183.6 5.2 %copy.35 = f32[4,2,2,512,128]{4,3,2,1,0:T(8,128)} copy(f32[4,2,2,512,128]{3,4,1,2,0:T(8,128)} %convolution_bitcast_fusion) | data formatting | bytes 8388608 | tf_op jit(solution)/shard_map/mk,kyzcn->yczmn/transpose | solution.py:47
  188.8 0.0 copy-start.1
  188.8 0.0 reduce-scatter.2.cloned.1.call-update
  188.9 39.2 %reduce-scatter.2.cloned.1.call-done = f32[1,2,512,128]{3,2,1,0:T(8,128)} async-done(((f32[8,2,512,128]{3,2,1,0:T(8,128)}), f32[1,2,512,128]{3,2,1,0:T(8,128)}) %reduce-scatter.2.cloned.1.call-update) | async-done | bytes 524304 | tf_op jit(solution)/shard_map/reduce_scatter | solution.py:49
  228.1 1.0 dynamic-slice_bitcast_fusion
  229.1 11.8 %collective-permute-start = (f32[512,128]{1,0:T(8,128)S(1)}, f32[512,128]{1,0:T(8,128)S(1)}, u32[]{:S(2)}, u32[]{:S(2)}) collective-permute-start(f32[512,128]{1,0:T(8,128)S(1)} %dynamic-slice_bitcast_fusion), channel_id=1, source_target_pairs={{0,2},{2,0},{1,3},{3,1},{4,6},{6,4},{5,7},{7,5},{8,10},{10,8},{9,1... | collective-permute-start | bytes 786440 | tf_op jit(solution)/shard_map/ppermute | solution.py:52
  240.9 0.0 copy-done.1
  240.9 0.2 compare_reduce_fusion
  241.0 0.1 broadcast_bitcast_fusion
  241.1 21.7 %collective-permute-done = f32[512,128]{1,0:T(8,128)S(1)} collective-permute-done((f32[512,128]{1,0:T(8,128)S(1)}, f32[512,128]{1,0:T(8,128)S(1)}, u32[]{:S(2)}, u32[]{:S(2)}) %collective-permute-start) | collective-permute-done | bytes 262176 | tf_op jit(solution)/shard_map/ppermute | solution.py:52
  262.8 1.8 fusion.2
  (7 shorter events, 0.0 us)
Async XLA Ops:
  6.5 53.5 %all-gather.7.cloned.1.call-start = ((), (), s32[]{:S(2)}) async-start(), calls=%async_computation.3 | async-start | bytes 1769472 | tf_op jit(solution)/shard_map/all_gather | solution.py:23
  25.1 152.2 %all-gather.5.cloned.1.call-start = ((), (), s32[]{:S(2)}) async-start(), calls=%async_computation.1 | async-start | bytes 4128768 | tf_op jit(solution)/shard_map/all_gather | solution.py:43
  66.5 13.3 %copy-start = (bf16[512,1024]{1,0:T(8,128)(2,1)S(1)}, bf16[512,1024]{1,0:T(8,128)(2,1)}, u32[]{:S(2)}) copy-start(bf16[512,1024]{1,0:T(8,128)(2,1)} %param.3) | copy-start | bytes 3145732
  79.8 148.3 %reduce-scatter.2.cloned.1.call-start = ((), (), s32[]{:S(2)}) async-start(), calls=%async_computation.2 | async-start | bytes 4718592 | tf_op jit(solution)/shard_map/reduce_scatter | solution.py:49
  188.8 52.0 %copy-start.1 = (s32[1,96]{1,0:T(1,128)S(1)}, s32[1,96]{1,0:T(1,128)}, u32[]{:S(2)}) copy-start(s32[1,96]{1,0:T(1,128)} %param.5) | copy-start | bytes 1156
  229.1 33.8 %collective-permute-start = (f32[512,128]{1,0:T(8,128)S(1)}, f32[512,128]{1,0:T(8,128)S(1)}, u32[]{:S(2)}, u32[]{:S(2)}) collective-permute-start(f32[512,128]{1,0:T(8,128)S(1)} %dynamic-slice_bitcast_fusion), channel_id=1, source_target_pairs={{0,2},{2,0},{1,3},{3,1},{4,6},{6,4},{5,7},{7,5},{8,10},{10,8},{9,1... | collective-permute-start | bytes 786440 | tf_op jit(solution)/shard_map/ppermute | solution.py:52
Sparse Core Ops, SparseCore 0:
  25.2 34.7 all-gather.6
  79.9 97.3 all-gather.4
  189.0 39.0 reduce-scatter.1

commit v4 on v3

--- a/solution.py
+++ b/solution.py
@@ -6,6 +6,7 @@
 BS = 128
 SBLK = 96
 CAP = 7
+SPLIT = 2
 ROW = ("zl", "x")
 COL = ("y", "zh", "c")
 
@@ -46,10 +47,15 @@
     rhs = expanded.reshape(-1, n_y, n_zh, n_c, chunk)
     partial_value = jnp.einsum("mk,kyzcn->yczmn", anc_kept, rhs, preferred_element_type=jnp.float32)
     partial_value = partial_value.reshape(n_y * n_c, n_zh, local_rows, chunk)
-    halves = lax.psum_scatter(partial_value, ("y", "c"), scatter_dimension=0, tiled=True)[0]
-    mine = lax.dynamic_index_in_dim(halves, zh_index, 0, keepdims=False)
-    other = lax.dynamic_index_in_dim(halves, 1 - zh_index, 0, keepdims=False)
-    summed = mine + lax.ppermute(other, "zh", [(0, 1), (1, 0)])
+    pieces = []
+    step = local_rows // SPLIT
+    for piece in range(SPLIT):
+        part = partial_value[:, :, piece * step:(piece + 1) * step]
+        halves = lax.psum_scatter(part, ("y", "c"), scatter_dimension=0, tiled=True)[0]
+        mine = lax.dynamic_index_in_dim(halves, zh_index, 0, keepdims=False)
+        other = lax.dynamic_index_in_dim(halves, 1 - zh_index, 0, keepdims=False)
+        pieces.append(mine + lax.ppermute(other, "zh", [(0, 1), (1, 0)]))
+    summed = jnp.concatenate(pieces, axis=0)
     member = jnp.any(blocks_of[None, :] == own_blocks[:, None], axis=1)
     row_mask = jnp.repeat(member, BS)
     results = [jnp.where(row_mask[:, None], -summed, jnp.zeros_like(summed))]

time: 272 us -> 304 us (1.12)
  waiting for transfers between devices: 189 us -> 203 us
  starting transfers between devices: 11.9 us -> 23.6 us
  local copies, waits for them, and re-layouts: 15.8 us -> 21.4 us
    reduce_scatter x1 -> x2, waiting for transfers between devices: 39.2 us -> 64.5 us  [body(): lax.psum_scatter(part, ('y', 'c'), scatter_dimension=0, tiled=True)[0]]
    ppermute x1 -> x2, waiting for transfers between devices: 21.7 us -> 10 us  [body(): pieces.append(mine + lax.ppermute(other, 'zh', [(0, 1), (1, 0)]))]
    ppermute x1 -> x2, starting transfers between devices: 11.8 us -> 23.4 us  [body(): pieces.append(mine + lax.ppermute(other, 'zh', [(0, 1), (1, 0)]))]
    slice x0 -> x1, local copies, waits for them, and re-layouts: none -> 4.65 us  [body(): part = partial_value[:, :, piece * step:(piece + 1) * step]]
  transfers between devices with their start and end apart: 4 -> 6, of which waited for: 4 -> 5; matrix products, arithmetic and copies ran while one was open for 2% -> 2% of each run, Pallas kernels for 0% -> 0%
where the time goes in v4:
time: 304 us
  waiting for transfers between devices  203 us (67%)
  blocking collectives  29.5 us (10%)
  starting transfers between devices  23.6 us (8%)
  local copies, waits for them, and re-layouts  21.4 us (7%)
  between operations  13.3 us (4%)
  matrix products  8.25 us (3%)
  other arithmetic  4.16 us (1%)
    all_gather x1, waiting for transfers between devices, body(): lax.all_gather(lax.all_gather(picked, 'x', axis=1, tiled=True), 'zl', axi...  94.6 us
    reduce_scatter x2, waiting for transfers between devices, body(): lax.psum_scatter(part, ('y', 'c'), scatter_dimension=0, tiled=True)[0]  64.5 us
    all_gather x1, waiting for transfers between devices, body(): gathered = lax.all_gather(gathered, ('y', 'c'), axis=0, tiled=True)  33.6 us
    ppermute x2, starting transfers between devices, body(): pieces.append(mine + lax.ppermute(other, 'zh', [(0, 1), (1, 0)]))  23.4 us
    all_gather x1, blocking collectives, body(): gathered = lax.all_gather(panel[0], 'zh', axis=0, tiled=True)  18.5 us
    all_gather x1, blocking collectives, body(): lax.all_gather(picked, 'x', axis=1, tiled=True)  11 us
    ppermute x2, waiting for transfers between devices, body(): pieces.append(mine + lax.ppermute(other, 'zh', [(0, 1), (1, 0)]))  10 us
    dot_general x1, matrix products, body(): jnp.einsum('mk,kyzcn->yczmn', anc_kept, rhs, preferred_element_type=jnp.f...  6.35 us
  transfers between devices with their start and end apart: 6, of which 5 were waited for; matrix products, arithmetic and copies ran while one was open for 2% of the time, Pallas kernels for 0%

profile of v4, /device:TPU:25, one launch (start us, length us, event | category | flops | bytes accessed | tf_op | source)
XLA Modules:
  0.0 303.5 jit_solution(4280800636657942676)
XLA Ops:
  6.5 0.0 all-gather.7.cloned.1.call-start
  6.5 18.5 %all-gather = bf16[1,1536,64]{1,2,0:T(8,128)(2,1)} all-gather(bf16[1,768,64]{1,2,0:T(8,128)(2,1)} %param.4), channel_id=2, replica_groups=mesh['zl'=8,'x'=4,'y'=4,'zh'=2,'c'=2] {'zh'}, dimensions={1}, use_global_device_ids=true | all-gather | bytes 294912 | tf_op jit(solution)/shard_map/all_gather | solution.py:23
  25.1 0.0 all-gather.7.cloned.1.call-update
  25.1 0.0 all-gather.5.cloned.1.call-start
  25.2 0.7 subtract_reduce_fusion
  25.8 0.1 sub.30
  25.9 0.1 sub.32
  26.0 0.1 fusion.3
  26.2 0.2 reduce-window.8
  26.4 33.6 %all-gather.7.cloned.1.call-done = bf16[1,12288,64]{1,2,0:T(8,128)(2,1)} async-done(((bf16[1,1536,64]{1,2,0:T(8,128)(2,1)}), bf16[1,12288,64]{1,2,0:T(8,128)(2,1)}) %all-gather.7.cloned.1.call-update) | async-done | bytes 1572880 | tf_op jit(solution)/shard_map/all_gather | solution.py:24
  60.0 3.1 %copy.29 = bf16[1,12288,64]{2,1,0:T(8,128)(2,1)S(1)} copy(bf16[1,12288,64]{1,2,0:T(8,128)(2,1)} %all-gather.7.cloned.1.call-done) | data formatting | bytes 3145728 | tf_op jit(solution)/shard_map/all_gather | solution.py:24
  63.1 3.5 %reshape.182 = bf16[96,8192]{1,0:T(8,128)(2,1)} reshape(bf16[1,12288,64]{2,1,0:T(8,128)(2,1)S(1)} %copy.29) | data formatting | bytes 3145728 | tf_op jit(solution)/shard_map/reshape | solution.py:29
  66.5 0.0 copy-start
  66.5 1.9 convolution_convert_fusion
  68.4 0.2 reshape.183
  68.7 0.1 copy.30
  68.8 11.0 %all_gather.14 = bf16[896,256]{0,1:T(8,128)(2,1)} all-gather(bf16[896,64]{0,1:T(8,128)(2,1)S(1)} %copy.30), channel_id=1, replica_groups=mesh['zl'=8,'x'=4,'y'=4,'zh'=2,'c'=2] {'x'}, dimensions={1}, use_global_device_ids=true | all-gather | bytes 573440 | tf_op jit(solution)/shard_map/all_gather | solution.py:44
  79.8 0.0 all-gather.5.cloned.1.call-update
  79.8 0.0 reduce-scatter.3.cloned.1.call-start
  79.8 0.0 copy-done
  79.9 0.5 copy.31
  80.4 0.7 copy.32
  81.1 0.1 select_reduce_fusion
  81.2 0.7 gather_fusion
  82.0 0.2 select_bitcast_fusion
  82.1 0.5 copy.33
  82.6 94.6 %all-gather.5.cloned.1.call-done = bf16[896,2048]{0,1:T(8,128)(2,1)} async-done(((bf16[896,256]{0,1:T(8,128)(2,1)}), bf16[896,2048]{0,1:T(8,128)(2,1)}) %all-gather.5.cloned.1.call-update) | async-done | bytes 3670032 | tf_op jit(solution)/shard_map/all_gather | solution.py:44
  177.3 6.3 %convolution_bitcast_fusion = f32[4,2,2,512,128]{3,4,1,2,0:T(8,128)} fusion(bf16[896,4,2,2,128]{0,4,3,2,1:T(8,128)(2,1)} %bitcast.45, bf16[512,896,1,1,1]{0,1,4,3,2:T(8,128)(2,1)S(1)} %bitcast.43), kind=kOutput, calls=%fused_computation.2 | convolution fusion | flops 1879048192 | bytes 8781824 | tf_op jit(solution)/shard_map/mk,kyzcn->yczmn/dot_general | solution.py:48
  183.6 5.2 %copy.35 = f32[4,2,2,512,128]{4,3,2,1,0:T(8,128)} copy(f32[4,2,2,512,128]{3,4,1,2,0:T(8,128)} %convolution_bitcast_fusion) | data formatting | bytes 8388608 | tf_op jit(solution)/shard_map/mk,kyzcn->yczmn/transpose | solution.py:48
  188.9 4.6 %fusion.14 = (f32[8,2,256,128]{3,2,1,0:T(8,128)}, f32[8,2,256,128]{3,2,1,0:T(8,128)}) fusion(f32[8,2,512,128]{3,2,1,0:T(8,128)} %bitcast.41), kind=kLoop, calls=%fused_computation.32 | loop fusion | bytes 8388608 | tf_op jit(solution)/shard_map/slice | solution.py:53
  193.5 0.0 copy-start.1
  193.5 0.0 reduce-scatter.3.cloned.1.call-update
  193.5 0.0 reduce-scatter.5.cloned.1.call-start
  193.6 0.5 reduce-scatter.5.cloned.1.call-update
  194.1 0.0 copy-done.1
  194.2 0.2 compare_reduce_fusion
  194.3 34.2 %reduce-scatter.3.cloned.1.call-done = f32[1,2,256,128]{3,2,1,0:T(8,128)} async-done(((f32[8,2,256,128]{3,2,1,0:T(8,128)}), f32[1,2,256,128]{3,2,1,0:T(8,128)}) %reduce-scatter.3.cloned.1.call-update) | async-done | bytes 262160 | tf_op jit(solution)/shard_map/reduce_scatter | solution.py:54
  228.6 0.9 dynamic-slice_bitcast_fusion.1
  229.5 11.7 %collective-permute-start = (f32[256,128]{1,0:T(8,128)S(1)}, f32[256,128]{1,0:T(8,128)S(1)}, u32[]{:S(2)}, u32[]{:S(2)}) collective-permute-start(f32[256,128]{1,0:T(8,128)S(1)} %dynamic-slice_bitcast_fusion.1), channel_id=1, source_target_pairs={{0,2},{2,0},{1,3},{3,1},{4,6},{6,4},{5,7},{7,5},{8,10},{10,8},{9,1... | collective-permute-start | bytes 393224 | tf_op jit(solution)/shard_map/ppermute | solution.py:57
  241.2 0.1 broadcast_bitcast_fusion
  241.2 30.3 %reduce-scatter.5.cloned.1.call-done = f32[1,2,256,128]{3,2,1,0:T(8,128)} async-done(((f32[8,2,256,128]{3,2,1,0:T(8,128)}), f32[1,2,256,128]{3,2,1,0:T(8,128)}) %reduce-scatter.5.cloned.1.call-update) | async-done | bytes 262160 | tf_op jit(solution)/shard_map/reduce_scatter | solution.py:54
  271.5 0.9 dynamic-slice_bitcast_fusion
  272.4 11.8 %collective-permute-start.1 = (f32[256,128]{1,0:T(8,128)S(1)}, f32[256,128]{1,0:T(8,128)S(1)}, u32[]{:S(2)}, u32[]{:S(2)}) collective-permute-start(f32[256,128]{1,0:T(8,128)S(1)} %dynamic-slice_bitcast_fusion), channel_id=1, source_target_pairs={{0,2},{2,0},{1,3},{3,1},{4,6},{6,4},{5,7},{7,5},{8,10},{10,8},{9,1... | collective-permute-start | bytes 393224 | tf_op jit(solution)/shard_map/ppermute | solution.py:57
  284.2 0.0 collective-permute-done
  284.3 0.9 fusion.2
  285.2 10.0 %collective-permute-done.1 = f32[256,128]{1,0:T(8,128)S(1)} collective-permute-done((f32[256,128]{1,0:T(8,128)S(1)}, f32[256,128]{1,0:T(8,128)S(1)}, u32[]{:S(2)}, u32[]{:S(2)}) %collective-permute-start.1) | collective-permute-done | bytes 131104 | tf_op jit(solution)/shard_map/ppermute | solution.py:57
  295.2 0.9 fusion.1
  296.1 0.8 fusion
  (7 shorter events, 0.0 us)
Async XLA Ops:
  6.5 53.5 %all-gather.7.cloned.1.call-start = ((), (), s32[]{:S(2)}) async-start(), calls=%async_computation.5 | async-start | bytes 1769472 | tf_op jit(solution)/shard_map/all_gather | solution.py:24
  25.1 152.2 %all-gather.5.cloned.1.call-start = ((), (), s32[]{:S(2)}) async-start(), calls=%async_computation.2 | async-start | bytes 4128768 | tf_op jit(solution)/shard_map/all_gather | solution.py:44
  66.5 13.3 %copy-start = (bf16[512,1024]{1,0:T(8,128)(2,1)S(1)}, bf16[512,1024]{1,0:T(8,128)(2,1)}, u32[]{:S(2)}) copy-start(bf16[512,1024]{1,0:T(8,128)(2,1)} %param.3) | copy-start | bytes 3145732
  79.8 148.8 %reduce-scatter.3.cloned.1.call-start = ((), (), s32[]{:S(2)}) async-start(), calls=%async_computation.3 | async-start | bytes 2359296 | tf_op jit(solution)/shard_map/reduce_scatter | solution.py:54
  193.5 0.7 copy-start.1
  193.5 78.0 %reduce-scatter.5.cloned.1.call-start = ((), (), s32[]{:S(2)}) async-start(), calls=%async_computation.4 | async-start | bytes 2359296 | tf_op jit(solution)/shard_map/reduce_scatter | solution.py:54
  229.5 54.7 %collective-permute-start = (f32[256,128]{1,0:T(8,128)S(1)}, f32[256,128]{1,0:T(8,128)S(1)}, u32[]{:S(2)}, u32[]{:S(2)}) collective-permute-start(f32[256,128]{1,0:T(8,128)S(1)} %dynamic-slice_bitcast_fusion.1), channel_id=1, source_target_pairs={{0,2},{2,0},{1,3},{3,1},{4,6},{6,4},{5,7},{7,5},{8,10},{10,8},{9,1... | collective-permute-start | bytes 393224 | tf_op jit(solution)/shard_map/ppermute | solution.py:57
  272.4 22.8 %collective-permute-start.1 = (f32[256,128]{1,0:T(8,128)S(1)}, f32[256,128]{1,0:T(8,128)S(1)}, u32[]{:S(2)}, u32[]{:S(2)}) collective-permute-start(f32[256,128]{1,0:T(8,128)S(1)} %dynamic-slice_bitcast_fusion), channel_id=1, source_target_pairs={{0,2},{2,0},{1,3},{3,1},{4,6},{6,4},{5,7},{7,5},{8,10},{10,8},{9,1... | collective-permute-start | bytes 393224 | tf_op jit(solution)/shard_map/ppermute | solution.py:57
Sparse Core Ops, SparseCore 0:
  25.2 34.7 all-gather.6
  79.9 97.3 all-gather.4
  193.7 34.8 reduce-scatter.2
  231.3 40.1 reduce-scatter.4

commit v5 on v3

--- a/solution.py
+++ b/solution.py
@@ -8,6 +8,35 @@
 CAP = 7
 ROW = ("zl", "x")
 COL = ("y", "zh", "c")
+
+
+def line_gather(v, axis, n):
+    i = lax.axis_index(axis)
+    right = [(j, j + 1) for j in range(n - 1)]
+    left = [(j + 1, j) for j in range(n - 1)]
+    from_left, from_right = [v], [v]
+    a = b = v
+    for _ in range(1, n):
+        a = lax.ppermute(a, axis, right)
+        b = lax.ppermute(b, axis, left)
+        from_left.append(a)
+        from_right.append(b)
+    j = jnp.arange(n)
+    got_left = jnp.take(jnp.stack(from_left), jnp.clip(i - j, 0, n - 1), axis=0)
+    got_right = jnp.take(jnp.stack(from_right), jnp.clip(j - i, 0, n - 1), axis=0)
+    return jnp.where((j <= i).reshape((n,) + (1,) * v.ndim), got_left, got_right)
+
+
+def ring_gather(w, axis, n):
+    i = lax.axis_index(axis)
+    fwd = [(j, (j + 1) % n) for j in range(n)]
+    bwd = [(j, (j - 1) % n) for j in range(n)]
+    a = lax.ppermute(w, axis, fwd)
+    b = lax.ppermute(w, axis, bwd)
+    h = w.shape[0] // 2
+    far = jnp.concatenate([lax.ppermute(a[:h], axis, fwd), lax.ppermute(b[h:], axis, bwd)])
+    by_offset = jnp.stack([w, a, far, b])
+    return jnp.take(by_offset, (i - jnp.arange(n)) % n, axis=0)
 
 
 def body(anc_inv, panel, structure):
@@ -40,12 +69,11 @@
         .reshape(CAP * BS, local_width)
     )
     anc_kept = jnp.take(anc_inv.reshape(local_rows, group_blocks, BS), slot_block, axis=1).reshape(local_rows, CAP * BS)
-    expanded = lax.all_gather(lax.all_gather(picked, "x", axis=1, tiled=True), "zl", axis=1, tiled=True)
-    width = expanded.shape[1]
-    chunk = width // (n_y * n_zh * n_c)
-    rhs = expanded.reshape(-1, n_y, n_zh, n_c, chunk)
-    partial_value = jnp.einsum("mk,kyzcn->yczmn", anc_kept, rhs, preferred_element_type=jnp.float32)
-    partial_value = partial_value.reshape(n_y * n_c, n_zh, local_rows, chunk)
+    n_zl, n_x = lax.axis_size("zl"), lax.axis_size("x")
+    pieces = ring_gather(line_gather(picked, "zl", n_zl), "x", n_x)
+    rhs = pieces.reshape(n_c, n_x // n_c, n_y, n_zh, CAP * BS, local_width)
+    partial_value = jnp.einsum("mk,cxyzkn->yczmxn", anc_kept, rhs, preferred_element_type=jnp.float32)
+    partial_value = partial_value.reshape(n_y * n_c, n_zh, local_rows, -1)
     halves = lax.psum_scatter(partial_value, ("y", "c"), scatter_dimension=0, tiled=True)[0]
     mine = lax.dynamic_index_in_dim(halves, zh_index, 0, keepdims=False)
     other = lax.dynamic_index_in_dim(halves, 1 - zh_index, 0, keepdims=False)

time: 272 us -> 298 us (1.096)
  waiting for transfers between devices: 189 us -> 129 us
  starting transfers between devices: 11.9 us -> 64.2 us
  local copies, waits for them, and re-layouts: 15.8 us -> 51.7 us
  other arithmetic: 3.26 us -> 15.4 us
  blocking collectives: 29.5 us -> 18.6 us
  matrix products: 8.21 us -> 4.19 us
    all_gather x1 -> x0, waiting for transfers between devices: 94.6 us -> none  [body(): lax.all_gather(lax.all_gather(picked, 'x', axis=1, tiled=True), 'zl', axi...]
    ppermute x0 -> x18, starting transfers between devices: none -> 52.3 us  [the longest x7 30.2 us: line_gather(): a = lax.ppermute(a, axis, right)]
    ppermute x0 -> x18, waiting for transfers between devices: none -> 19.1 us  [the longest x1 8.5 us: ring_gather(): a = lax.ppermute(w, axis, fwd)]
    reduce_scatter x1, waiting for transfers between devices: 39.2 us -> 55.2 us  [body(): lax.psum_scatter(partial_value, ('y', 'c'), scatter_dimension=0, tiled=True)]
    gather x0 -> x3, local copies, waits for them, and re-layouts: none -> 13.1 us  [the longest x1 7.57 us: ring_gather(): return jnp.take(by_offset, (i - jnp.arange(n)) % n, axis=0)]
    all_gather x1 -> x0, blocking collectives: 11 us -> none  [body(): lax.all_gather(picked, 'x', axis=1, tiled=True)]
    ppermute x0 -> x4, local copies, waits for them, and re-layouts: none -> 8.95 us  [the longest x1 2.65 us: ring_gather(): a = lax.ppermute(w, axis, fwd)]
    unnamed x5 -> x23, local copies, waits for them, and re-layouts: 0.55 us -> 7.79 us
  transfers between devices with their start and end apart: 4 -> 21, of which waited for: 4 -> 15; matrix products, arithmetic and copies ran while one was open for 2% -> 10% of each run, Pallas kernels for 0% -> 0%
where the time goes in v5:
time: 298 us; the launch traced here: 297 us
  waiting for transfers between devices  129 us (43%)
  starting transfers between devices  64.2 us (22%)
  local copies, waits for them, and re-layouts  51.7 us (17%)
  blocking collectives  18.6 us (6%)
  other arithmetic  15.4 us (5%)
  between operations  13.9 us (5%)
  matrix products  4.19 us (1%)
    reduce_scatter x1, waiting for transfers between devices, body(): lax.psum_scatter(partial_value, ('y', 'c'), scatter_dimension=0, tiled=True)  55.2 us
    all_gather x1, waiting for transfers between devices, body(): gathered = lax.all_gather(gathered, ('y', 'c'), axis=0, tiled=True)  33.5 us
    ppermute x7, starting transfers between devices, line_gather(): a = lax.ppermute(a, axis, right)  30.2 us
    ppermute x1, waiting for transfers between devices, body(): summed = mine + lax.ppermute(other, 'zh', [(0, 1), (1, 0)])  21.5 us
    all_gather x1, blocking collectives, body(): gathered = lax.all_gather(panel[0], 'zh', axis=0, tiled=True)  18.6 us
    ppermute x1, starting transfers between devices, body(): summed = mine + lax.ppermute(other, 'zh', [(0, 1), (1, 0)])  11.9 us
    ppermute x7, starting transfers between devices, line_gather(): b = lax.ppermute(b, axis, left)  8.99 us
    ppermute x1, waiting for transfers between devices, ring_gather(): a = lax.ppermute(w, axis, fwd)  8.5 us
  transfers between devices with their start and end apart: 21, of which 15 were waited for; matrix products, arithmetic and copies ran while one was open for 10% of the time, Pallas kernels for 0%

profile of v5, /device:TPU:25, one launch (start us, length us, event | category | flops | bytes accessed | tf_op | source)
XLA Modules:
  0.0 297.3 jit_solution(13529151546148338864)
XLA Ops:
  6.5 18.6 %all-gather = bf16[1,1536,64]{1,2,0:T(8,128)(2,1)} all-gather(bf16[1,768,64]{1,2,0:T(8,128)(2,1)} %param.6), channel_id=2, replica_groups=mesh['zl'=8,'x'=4,'y'=4,'zh'=2,'c'=2] {'zh'}, dimensions={1}, use_global_device_ids=true | all-gather | bytes 294912 | tf_op jit(solution)/shard_map/all_gather | solution.py:51
  26.5 33.5 %all-gather.4.cloned.1.call-done = bf16[1,12288,64]{1,2,0:T(8,128)(2,1)} async-done(((bf16[1,1536,64]{1,2,0:T(8,128)(2,1)}), bf16[1,12288,64]{1,2,0:T(8,128)(2,1)}) %all-gather.4.cloned.1.call-update) | async-done | bytes 1572880 | tf_op jit(solution)/shard_map/all_gather | solution.py:52
  60.0 3.1 %copy.39 = bf16[1,12288,64]{2,1,0:T(8,128)(2,1)S(1)} copy(bf16[1,12288,64]{1,2,0:T(8,128)(2,1)} %all-gather.4.cloned.1.call-done) | data formatting | bytes 3145728 | tf_op jit(solution)/shard_map/all_gather | solution.py:52
  63.1 3.5 %reshape.200 = bf16[96,8192]{1,0:T(8,128)(2,1)} reshape(bf16[1,12288,64]{2,1,0:T(8,128)(2,1)S(1)} %copy.39) | data formatting | bytes 3145728 | tf_op jit(solution)/shard_map/reshape | solution.py:57
  66.5 1.8 convolution_convert_fusion
  68.8 3.1 %collective-permute-start = (bf16[896,64]{1,0:T(8,128)(2,1)S(1)}, bf16[896,64]{1,0:T(8,128)(2,1)S(1)}, u32[]{:S(2)}, u32[]{:S(2)}) collective-permute-start(bf16[896,64]{1,0:T(8,128)(2,1)S(1)} %reshape.201), channel_id=1, source_target_pairs={{0,64},{64,128},{128,192},{192,256},{256,320},{320,384},{384,448},... | collective-permute-start | bytes 344072 | tf_op jit(solution)/shard_map/ppermute | solution.py:20
  71.9 1.3 collective-permute-start.7
  73.2 1.2 copy.64
  74.5 2.1 collective-permute-done
  76.6 4.1 %collective-permute-start.1 = (bf16[896,64]{1,0:T(8,128)(2,1)S(1)}, bf16[896,64]{1,0:T(8,128)(2,1)S(1)}, u32[]{:S(2)}, u32[]{:S(2)}) collective-permute-start(bf16[896,64]{1,0:T(8,128)(2,1)S(1)} %collective-permute-done), channel_id=1, source_target_pairs={{0,64},{64,128},{128,192},{192,256},{256,320},{320,384},{384,448},... | collective-permute-start | bytes 344072 | tf_op jit(solution)/shard_map/ppermute | solution.py:20
  80.7 0.7 bitcast_dynamic-update-slice_fusion.13
  81.5 1.3 collective-permute-start.8
  82.8 1.7 collective-permute-done.1
  84.5 4.1 %collective-permute-start.2 = (bf16[896,64]{1,0:T(8,128)(2,1)S(1)}, bf16[896,64]{1,0:T(8,128)(2,1)S(1)}, u32[]{:S(2)}, u32[]{:S(2)}) collective-permute-start(bf16[896,64]{1,0:T(8,128)(2,1)S(1)} %collective-permute-done.1), channel_id=1, source_target_pairs={{0,64},{64,128},{128,192},{192,256},{256,320},{320,384},{384,448},... | collective-permute-start | bytes 344072 | tf_op jit(solution)/shard_map/ppermute | solution.py:20
  89.3 1.3 collective-permute-start.9
  90.6 0.9 collective-permute-done.2
  91.5 3.8 %collective-permute-start.3 = (bf16[896,64]{1,0:T(8,128)(2,1)S(1)}, bf16[896,64]{1,0:T(8,128)(2,1)S(1)}, u32[]{:S(2)}, u32[]{:S(2)}) collective-permute-start(bf16[896,64]{1,0:T(8,128)(2,1)S(1)} %collective-permute-done.2), channel_id=1, source_target_pairs={{0,64},{64,128},{128,192},{192,256},{256,320},{320,384},{384,448},... | collective-permute-start | bytes 344072 | tf_op jit(solution)/shard_map/ppermute | solution.py:20
  95.4 0.7 bitcast_dynamic-update-slice_fusion.11
  96.1 1.3 collective-permute-start.10
  97.4 0.9 collective-permute-done.3
  98.3 5.5 %collective-permute-start.4 = (bf16[896,64]{1,0:T(8,128)(2,1)S(1)}, bf16[896,64]{1,0:T(8,128)(2,1)S(1)}, u32[]{:S(2)}, u32[]{:S(2)}) collective-permute-start(bf16[896,64]{1,0:T(8,128)(2,1)S(1)} %collective-permute-done.3), channel_id=1, source_target_pairs={{0,64},{64,128},{128,192},{192,256},{256,320},{320,384},{384,448},... | collective-permute-start | bytes 344072 | tf_op jit(solution)/shard_map/ppermute | solution.py:20
  103.8 0.7 bitcast_dynamic-update-slice_fusion.10
  105.2 1.3 collective-permute-start.11
  106.7 4.5 %collective-permute-start.5 = (bf16[896,64]{1,0:T(8,128)(2,1)S(1)}, bf16[896,64]{1,0:T(8,128)(2,1)S(1)}, u32[]{:S(2)}, u32[]{:S(2)}) collective-permute-start(bf16[896,64]{1,0:T(8,128)(2,1)S(1)} %collective-permute-done.4), channel_id=1, source_target_pairs={{0,64},{64,128},{128,192},{192,256},{256,320},{320,384},{384,448},... | collective-permute-start | bytes 344072 | tf_op jit(solution)/shard_map/ppermute | solution.py:20
  111.2 0.7 bitcast_dynamic-update-slice_fusion.9
  111.9 0.7 collective-permute-done.11
  112.6 1.3 collective-permute-start.12
  114.2 5.0 %collective-permute-start.6 = (bf16[896,64]{1,0:T(8,128)(2,1)S(1)}, bf16[896,64]{1,0:T(8,128)(2,1)S(1)}, u32[]{:S(2)}, u32[]{:S(2)}) collective-permute-start(bf16[896,64]{1,0:T(8,128)(2,1)S(1)} %collective-permute-done.5), channel_id=1, source_target_pairs={{0,64},{64,128},{128,192},{192,256},{256,320},{320,384},{384,448},... | collective-permute-start | bytes 344072 | tf_op jit(solution)/shard_map/ppermute | solution.py:20
  119.2 0.7 bitcast_dynamic-update-slice_fusion.8
  119.9 0.7 collective-permute-done.12
  120.6 1.3 collective-permute-start.13
  122.2 0.7 bitcast_dynamic-update-slice_fusion.7
  122.9 3.6 %gather_fusion.2 = bf16[8,896,64]{2,1,0:T(8,128)(2,1)} fusion(bf16[8,896,64]{2,1,0:T(8,128)(2,1)} %bitcast_dynamic-update-slice_fusion.7, s32[1024]{0:T(1024)S(1)} %get-tuple-element.11), kind=kCustom, calls=%fused_computation.clone | custom fusion | bytes 1835040 | tf_op jit(solution)/shard_map/jit(_take)/gather | solution.py:25
  126.4 2.2 collective-permute-done.13
  128.6 2.0 gather_fusion.3
  130.7 2.4 select_select_fusion
  133.1 1.5 copy.40
  134.6 3.1 %collective-permute-start.14 = (bf16[8,896,64]{1,2,0:T(8,128)(2,1)}, bf16[8,896,64]{1,2,0:T(8,128)(2,1)}, u32[]{:S(2)}, u32[]{:S(2)}) collective-permute-start(bf16[8,896,64]{1,2,0:T(8,128)(2,1)} %copy.40), channel_id=1, source_target_pairs={{0,16},{16,32},{32,48},{48,0},{1,17},{17,33},{33,49},{49,1},{2,18}... | collective-permute-start | bytes 2752520 | tf_op jit(solution)/shard_map/ppermute | solution.py:34
  137.7 3.4 %collective-permute-start.16 = (bf16[8,896,64]{1,2,0:T(8,128)(2,1)}, bf16[8,896,64]{1,2,0:T(8,128)(2,1)}, u32[]{:S(2)}, u32[]{:S(2)}) collective-permute-start(bf16[8,896,64]{1,2,0:T(8,128)(2,1)} %copy.40), channel_id=1, source_target_pairs={{0,48},{16,0},{32,16},{48,32},{1,49},{17,1},{33,17},{49,33},{2,50}... | collective-permute-start | bytes 2752520 | tf_op jit(solution)/shard_map/ppermute | solution.py:35
  141.1 1.5 copy.46
  142.6 1.3 copy.47
  144.1 8.5 %collective-permute-done.14 = bf16[8,896,64]{1,2,0:T(8,128)(2,1)} collective-permute-done((bf16[8,896,64]{1,2,0:T(8,128)(2,1)}, bf16[8,896,64]{1,2,0:T(8,128)(2,1)}, u32[]{:S(2)}, u32[]{:S(2)}) %collective-permute-start.14) | collective-permute-done | bytes 917536 | tf_op jit(solution)/shard_map/ppermute | solution.py:34
  152.6 1.1 slice.16
  153.6 1.9 collective-permute-start.15
  155.6 1.8 slice.17
  157.4 4.7 %collective-permute-start.17 = (bf16[4,896,64]{1,2,0:T(8,128)(2,1)}, bf16[4,896,64]{1,2,0:T(8,128)(2,1)}, u32[]{:S(2)}, u32[]{:S(2)}) collective-permute-start(bf16[4,896,64]{1,2,0:T(8,128)(2,1)} %slice.17), channel_id=1, source_target_pairs={{0,48},{16,0},{32,16},{48,32},{1,49},{17,1},{33,17},{49,33},{2,50}... | collective-permute-start | bytes 1376264 | tf_op jit(solution)/shard_map/ppermute | solution.py:37
  162.2 1.9 gather_fusion.1
  164.1 1.1 select_bitcast_fusion
  165.2 2.3 copy.48
  167.5 2.7 copy.41
  170.2 2.6 copy.45
  172.8 1.4 copy.43
  174.2 2.3 copy.44
  176.5 1.7 maximum_bitcast_fusion
  178.8 4.1 %pad_maximum_fusion = bf16[4,8,896,64]{3,2,1,0:T(8,128)(2,1)} fusion(bf16[1,8,896,64]{3,2,1,0:T(8,128)(2,1)S(1)} %bitcast.75, bf16[1,8,896,64]{3,2,1,0:T(8,128)(2,1)S(1)} %maximum_bitcast_fusion, bf16[1,8,896,64]{3,2,1,0:T(8,128)(2,1)S(1)} %bitcast.74, bf16[1,8,896,64]{3,2,1,0:T(8,128)(2,1)S(1)} %bitcast.73), kind=kLoop, calls=%fused_computation.5 | loop fusion | flops 5505024 | bytes 7340032 | tf_op jit(solution)/shard_map/stack | solution.py:38
  182.9 7.6 %gather_fusion = bf16[4,8,896,64]{3,2,1,0:T(8,128)(2,1)} fusion(bf16[4,8,896,64]{3,2,1,0:T(8,128)(2,1)} %pad_maximum_fusion, s32[1024]{0:T(1024)S(1)} %get-tuple-element.13), kind=kCustom, calls=%fused_computation.2 | custom fusion | bytes 7340048 | tf_op jit(solution)/shard_map/jit(_take)/gather | solution.py:39
  190.5 3.9 %broadcast_select_fusion = bf16[4,8,896,64]{3,2,1,0:T(8,128)(2,1)S(1)} fusion(bf16[4,8,896,64]{3,2,1,0:T(8,128)(2,1)} %gather_fusion, pred[4]{0:T(512)(128)(4,1)S(1)} %compare_and_fusion.3), kind=kLoop, calls=%fused_computation.6 | loop fusion | flops 1835008 | bytes 7340036 | tf_op jit(solution)/shard_map/jit(_take)/select_n | solution.py:39
  194.5 2.4 convolution_bitcast_fusion
  196.8 2.5 copy.51
  199.4 55.2 %reduce-scatter.2.cloned.1.call-done = f32[1,2,512,128]{2,3,1,0:T(8,128)} async-done(((f32[8,2,512,128]{2,3,1,0:T(8,128)}), f32[1,2,512,128]{2,3,1,0:T(8,128)}) %reduce-scatter.2.cloned.1.call-update) | async-done | bytes 524304 | tf_op jit(solution)/shard_map/reduce_scatter | solution.py:77
  254.7 1.1 constant_dynamic-slice_fusion.1
  255.9 11.9 %collective-permute-start.18 = (f32[512,128]{1,0:T(8,128)S(1)}, f32[512,128]{1,0:T(8,128)S(1)}, u32[]{:S(2)}, u32[]{:S(2)}) collective-permute-start(f32[512,128]{1,0:T(8,128)S(1)} %bitcast.78), channel_id=1, source_target_pairs={{0,2},{2,0},{1,3},{3,1},{4,6},{6,4},{5,7},{7,5},{8,10},{10,8},{9,1... | collective-permute-start | bytes 786440 | tf_op jit(solution)/shard_map/ppermute | solution.py:80
  268.1 21.5 %collective-permute-done.18 = f32[512,128]{1,0:T(8,128)S(1)} collective-permute-done((f32[512,128]{1,0:T(8,128)S(1)}, f32[512,128]{1,0:T(8,128)S(1)}, u32[]{:S(2)}, u32[]{:S(2)}) %collective-permute-start.18) | collective-permute-done | bytes 262176 | tf_op jit(solution)/shard_map/ppermute | solution.py:80
  289.6 0.8 fusion.2
  (57 shorter events, 5.3 us)
Async XLA Ops:
  6.5 53.5 %all-gather.4.cloned.1.call-start = ((), (), s32[]{:S(2)}) async-start(), calls=%async_computation.2 | async-start | bytes 1769472 | tf_op jit(solution)/shard_map/all_gather | solution.py:52
  25.1 229.5 %reduce-scatter.2.cloned.1.call-start = ((), (), s32[]{:S(2)}) async-start(), calls=%async_computation.1 | async-start | bytes 4718592 | tf_op jit(solution)/shard_map/reduce_scatter | solution.py:77
  68.8 7.8 %collective-permute-start = (bf16[896,64]{1,0:T(8,128)(2,1)S(1)}, bf16[896,64]{1,0:T(8,128)(2,1)S(1)}, u32[]{:S(2)}, u32[]{:S(2)}) collective-permute-start(bf16[896,64]{1,0:T(8,128)(2,1)S(1)} %reshape.201), channel_id=1, source_target_pairs={{0,64},{64,128},{128,192},{192,256},{256,320},{320,384},{384,448},... | collective-permute-start | bytes 344072 | tf_op jit(solution)/shard_map/ppermute | solution.py:20
  71.9 9.5 %collective-permute-start.7 = (bf16[896,64]{1,0:T(8,128)(2,1)S(1)}, bf16[896,64]{1,0:T(8,128)(2,1)S(1)}, u32[]{:S(2)}, u32[]{:S(2)}) collective-permute-start(bf16[896,64]{1,0:T(8,128)(2,1)S(1)} %reshape.201), channel_id=1, source_target_pairs={{64,0},{128,64},{192,128},{256,192},{320,256},{384,320},{448,384},... | collective-permute-start | bytes 344072 | tf_op jit(solution)/shard_map/ppermute | solution.py:21
  76.6 7.9 %collective-permute-start.1 = (bf16[896,64]{1,0:T(8,128)(2,1)S(1)}, bf16[896,64]{1,0:T(8,128)(2,1)S(1)}, u32[]{:S(2)}, u32[]{:S(2)}) collective-permute-start(bf16[896,64]{1,0:T(8,128)(2,1)S(1)} %collective-permute-done), channel_id=1, source_target_pairs={{0,64},{64,128},{128,192},{192,256},{256,320},{320,384},{384,448},... | collective-permute-start | bytes 344072 | tf_op jit(solution)/shard_map/ppermute | solution.py:20
  81.5 7.8 %collective-permute-start.8 = (bf16[896,64]{1,0:T(8,128)(2,1)S(1)}, bf16[896,64]{1,0:T(8,128)(2,1)S(1)}, u32[]{:S(2)}, u32[]{:S(2)}) collective-permute-start(bf16[896,64]{1,0:T(8,128)(2,1)S(1)} %collective-permute-done.7), channel_id=1, source_target_pairs={{64,0},{128,64},{192,128},{256,192},{320,256},{384,320},{448,384},... | collective-permute-start | bytes 344072 | tf_op jit(solution)/shard_map/ppermute | solution.py:21
  84.5 7.0 %collective-permute-start.2 = (bf16[896,64]{1,0:T(8,128)(2,1)S(1)}, bf16[896,64]{1,0:T(8,128)(2,1)S(1)}, u32[]{:S(2)}, u32[]{:S(2)}) collective-permute-start(bf16[896,64]{1,0:T(8,128)(2,1)S(1)} %collective-permute-done.1), channel_id=1, source_target_pairs={{0,64},{64,128},{128,192},{192,256},{256,320},{320,384},{384,448},... | collective-permute-start | bytes 344072 | tf_op jit(solution)/shard_map/ppermute | solution.py:20
  89.3 6.8 %collective-permute-start.9 = (bf16[896,64]{1,0:T(8,128)(2,1)S(1)}, bf16[896,64]{1,0:T(8,128)(2,1)S(1)}, u32[]{:S(2)}, u32[]{:S(2)}) collective-permute-start(bf16[896,64]{1,0:T(8,128)(2,1)S(1)} %collective-permute-done.8), channel_id=1, source_target_pairs={{64,0},{128,64},{192,128},{256,192},{320,256},{384,320},{448,384},... | collective-permute-start | bytes 344072 | tf_op jit(solution)/shard_map/ppermute | solution.py:21
  91.5 6.8 %collective-permute-start.3 = (bf16[896,64]{1,0:T(8,128)(2,1)S(1)}, bf16[896,64]{1,0:T(8,128)(2,1)S(1)}, u32[]{:S(2)}, u32[]{:S(2)}) collective-permute-start(bf16[896,64]{1,0:T(8,128)(2,1)S(1)} %collective-permute-done.2), channel_id=1, source_target_pairs={{0,64},{64,128},{128,192},{192,256},{256,320},{320,384},{384,448},... | collective-permute-start | bytes 344072 | tf_op jit(solution)/shard_map/ppermute | solution.py:20
  96.1 9.2 %collective-permute-start.10 = (bf16[896,64]{1,0:T(8,128)(2,1)S(1)}, bf16[896,64]{1,0:T(8,128)(2,1)S(1)}, u32[]{:S(2)}, u32[]{:S(2)}) collective-permute-start(bf16[896,64]{1,0:T(8,128)(2,1)S(1)} %collective-permute-done.9), channel_id=1, source_target_pairs={{64,0},{128,64},{192,128},{256,192},{320,256},{384,320},{448,384},... | collective-permute-start | bytes 344072 | tf_op jit(solution)/shard_map/ppermute | solution.py:21
  98.3 8.5 %collective-permute-start.4 = (bf16[896,64]{1,0:T(8,128)(2,1)S(1)}, bf16[896,64]{1,0:T(8,128)(2,1)S(1)}, u32[]{:S(2)}, u32[]{:S(2)}) collective-permute-start(bf16[896,64]{1,0:T(8,128)(2,1)S(1)} %collective-permute-done.3), channel_id=1, source_target_pairs={{0,64},{64,128},{128,192},{192,256},{256,320},{320,384},{384,448},... | collective-permute-start | bytes 344072 | tf_op jit(solution)/shard_map/ppermute | solution.py:20
  105.2 7.4 %collective-permute-start.11 = (bf16[896,64]{1,0:T(8,128)(2,1)S(1)}, bf16[896,64]{1,0:T(8,128)(2,1)S(1)}, u32[]{:S(2)}, u32[]{:S(2)}) collective-permute-start(bf16[896,64]{1,0:T(8,128)(2,1)S(1)} %collective-permute-done.10), channel_id=1, source_target_pairs={{64,0},{128,64},{192,128},{256,192},{320,256},{384,320},{448,384},... | collective-permute-start | bytes 344072 | tf_op jit(solution)/shard_map/ppermute | solution.py:21
  106.7 7.4 %collective-permute-start.5 = (bf16[896,64]{1,0:T(8,128)(2,1)S(1)}, bf16[896,64]{1,0:T(8,128)(2,1)S(1)}, u32[]{:S(2)}, u32[]{:S(2)}) collective-permute-start(bf16[896,64]{1,0:T(8,128)(2,1)S(1)} %collective-permute-done.4), channel_id=1, source_target_pairs={{0,64},{64,128},{128,192},{192,256},{256,320},{320,384},{384,448},... | collective-permute-start | bytes 344072 | tf_op jit(solution)/shard_map/ppermute | solution.py:20
  112.6 8.0 %collective-permute-start.12 = (bf16[896,64]{1,0:T(8,128)(2,1)S(1)}, bf16[896,64]{1,0:T(8,128)(2,1)S(1)}, u32[]{:S(2)}, u32[]{:S(2)}) collective-permute-start(bf16[896,64]{1,0:T(8,128)(2,1)S(1)} %collective-permute-done.11), channel_id=1, source_target_pairs={{64,0},{128,64},{192,128},{256,192},{320,256},{384,320},{448,384},... | collective-permute-start | bytes 344072 | tf_op jit(solution)/shard_map/ppermute | solution.py:21
  114.2 8.0 %collective-permute-start.6 = (bf16[896,64]{1,0:T(8,128)(2,1)S(1)}, bf16[896,64]{1,0:T(8,128)(2,1)S(1)}, u32[]{:S(2)}, u32[]{:S(2)}) collective-permute-start(bf16[896,64]{1,0:T(8,128)(2,1)S(1)} %collective-permute-done.5), channel_id=1, source_target_pairs={{0,64},{64,128},{128,192},{192,256},{256,320},{320,384},{384,448},... | collective-permute-start | bytes 344072 | tf_op jit(solution)/shard_map/ppermute | solution.py:20
  120.6 8.0 %collective-permute-start.13 = (bf16[896,64]{1,0:T(8,128)(2,1)S(1)}, bf16[896,64]{1,0:T(8,128)(2,1)S(1)}, u32[]{:S(2)}, u32[]{:S(2)}) collective-permute-start(bf16[896,64]{1,0:T(8,128)(2,1)S(1)} %collective-permute-done.12), channel_id=1, source_target_pairs={{64,0},{128,64},{192,128},{256,192},{320,256},{384,320},{448,384},... | collective-permute-start | bytes 344072 | tf_op jit(solution)/shard_map/ppermute | solution.py:21
  134.6 18.0 %collective-permute-start.14 = (bf16[8,896,64]{1,2,0:T(8,128)(2,1)}, bf16[8,896,64]{1,2,0:T(8,128)(2,1)}, u32[]{:S(2)}, u32[]{:S(2)}) collective-permute-start(bf16[8,896,64]{1,2,0:T(8,128)(2,1)} %copy.40), channel_id=1, source_target_pairs={{0,16},{16,32},{32,48},{48,0},{1,17},{17,33},{33,49},{49,1},{2,18}... | collective-permute-start | bytes 2752520 | tf_op jit(solution)/shard_map/ppermute | solution.py:34
  137.7 17.9 %collective-permute-start.16 = (bf16[8,896,64]{1,2,0:T(8,128)(2,1)}, bf16[8,896,64]{1,2,0:T(8,128)(2,1)}, u32[]{:S(2)}, u32[]{:S(2)}) collective-permute-start(bf16[8,896,64]{1,2,0:T(8,128)(2,1)} %copy.40), channel_id=1, source_target_pairs={{0,48},{16,0},{32,16},{48,32},{1,49},{17,1},{33,17},{49,33},{2,50}... | collective-permute-start | bytes 2752520 | tf_op jit(solution)/shard_map/ppermute | solution.py:35
  153.6 19.1 %collective-permute-start.15 = (bf16[4,896,64]{1,2,0:T(8,128)(2,1)S(1)}, bf16[4,896,64]{1,2,0:T(8,128)(2,1)}, u32[]{:S(2)}, u32[]{:S(2)}) collective-permute-start(bf16[4,896,64]{1,2,0:T(8,128)(2,1)S(1)} %slice.16), channel_id=1, source_target_pairs={{0,16},{16,32},{32,48},{48,0},{1,17},{17,33},{33,49},{49,1},{2,18}... | collective-permute-start | bytes 1376264 | tf_op jit(solution)/shard_map/ppermute | solution.py:37
  157.4 16.8 %collective-permute-start.17 = (bf16[4,896,64]{1,2,0:T(8,128)(2,1)}, bf16[4,896,64]{1,2,0:T(8,128)(2,1)}, u32[]{:S(2)}, u32[]{:S(2)}) collective-permute-start(bf16[4,896,64]{1,2,0:T(8,128)(2,1)} %slice.17), channel_id=1, source_target_pairs={{0,48},{16,0},{32,16},{48,32},{1,49},{17,1},{33,17},{49,33},{2,50}... | collective-permute-start | bytes 1376264 | tf_op jit(solution)/shard_map/ppermute | solution.py:37
  176.5 1.8 copy-start
  176.5 2.3 copy-start.1
  190.5 3.9 %copy-start.2 = (bf16[512,7,128]{0,2,1:T(8,128)(2,1)S(1)}, bf16[512,7,128]{0,2,1:T(8,128)(2,1)}, u32[]{:S(2)}) copy-start(bf16[512,7,128]{0,2,1:T(8,128)(2,1)} %copy.48) | copy-start | bytes 2752516
  199.4 68.3 %copy-start.3 = (s32[1,96]{1,0:T(1,128)S(1)}, s32[1,96]{1,0:T(1,128)}, u32[]{:S(2)}) copy-start(s32[1,96]{1,0:T(1,128)} %param.7) | copy-start | bytes 1156
  255.9 33.8 %collective-permute-start.18 = (f32[512,128]{1,0:T(8,128)S(1)}, f32[512,128]{1,0:T(8,128)S(1)}, u32[]{:S(2)}, u32[]{:S(2)}) collective-permute-start(f32[512,128]{1,0:T(8,128)S(1)} %bitcast.78), channel_id=1, source_target_pairs={{0,2},{2,0},{1,3},{3,1},{4,6},{6,4},{5,7},{7,5},{8,10},{10,8},{9,1... | collective-permute-start | bytes 786440 | tf_op jit(solution)/shard_map/ppermute | solution.py:80
Sparse Core Ops, SparseCore 0:
  25.3 34.6 all-gather.3
  199.5 55.0 reduce-scatter.1

commit v6 on v3

--- a/solution.py
+++ b/solution.py
@@ -19,26 +19,33 @@
     group_blocks = local_cols // BS
     local_width = panel.shape[2]
     per_dev = panel.shape[1] // BS
-    gathered = lax.all_gather(panel[0], "zh", axis=0, tiled=True)
-    gathered = lax.all_gather(gathered, ("y", "c"), axis=0, tiled=True)
+    y_index, c_index = lax.axis_index("y"), lax.axis_index("c")
     blocks_of = structure[0]
-    blocks_gathered = blocks_of.reshape(n_y, n_zh, n_c, per_dev).transpose(0, 2, 1, 3).reshape(SBLK)
     own_blocks = row_index * (local_rows // BS) + jnp.arange(local_rows // BS, dtype=jnp.int32)
     block_ids = jnp.arange(group_blocks, dtype=jnp.int32)
-    compact = gathered.reshape(SBLK, BS * local_width)
-    local_block = blocks_gathered - col_index * group_blocks
+    held = lax.all_gather(panel[0], "zh", axis=0, tiled=True).reshape(n_zh * per_dev, BS * local_width)
+    by_col = blocks_of.reshape(n_y, n_zh, n_c, per_dev)
+    held_blocks = lax.dynamic_index_in_dim(lax.dynamic_index_in_dim(by_col, y_index, 0, False), c_index, 1, False)
+    held_blocks = held_blocks.reshape(n_zh * per_dev)
+    same_group = (held_blocks[:, None] // group_blocks) == (blocks_of[None, :] // group_blocks)
+    slot = jnp.sum(same_group & (blocks_of[None, :] < held_blocks[:, None]), axis=1)
+    dest_y = jnp.arange(n_y, dtype=jnp.int32)[:, None]
+    dest_c = jnp.arange(n_c, dtype=jnp.int32)[None, :]
+    dest_col = ((dest_y * n_zh + zh_index) * n_c + dest_c).reshape(n_y * n_c)
+    slot_ids = jnp.arange(CAP, dtype=jnp.int32)
+    placer = (
+        ((held_blocks // group_blocks)[None, None, :] == dest_col[:, None, None])
+        & (slot[None, None, :] == slot_ids[None, :, None])
+    ).astype(jnp.bfloat16)
+    placed = jnp.einsum("djq,qf->djf", placer, held, preferred_element_type=jnp.float32).astype(jnp.bfloat16)
+    picked = lax.psum_scatter(placed, ("y", "c"), scatter_dimension=0, tiled=True)[0]
+    picked = picked.reshape(CAP * BS, local_width)
+    local_block = blocks_of - col_index * group_blocks
     hits = local_block[None, :] == block_ids[:, None]
     present = jnp.any(hits, axis=1)
     rank = jnp.cumsum(present.astype(jnp.int32)) - 1
-    slot_ids = jnp.arange(CAP, dtype=jnp.int32)
     slot_of = present[None, :] & (rank[None, :] == slot_ids[:, None])
-    picker = jnp.dot(slot_of.astype(jnp.float32), hits.astype(jnp.float32)).astype(jnp.bfloat16)
     slot_block = jnp.sum(jnp.where(slot_of, block_ids[None, :], 0), axis=1)
-    picked = (
-        jnp.dot(picker, compact, preferred_element_type=jnp.float32)
-        .astype(jnp.bfloat16)
-        .reshape(CAP * BS, local_width)
-    )
     anc_kept = jnp.take(anc_inv.reshape(local_rows, group_blocks, BS), slot_block, axis=1).reshape(local_rows, CAP * BS)
     expanded = lax.all_gather(lax.all_gather(picked, "x", axis=1, tiled=True), "zl", axis=1, tiled=True)
     width = expanded.shape[1]

time: 272 us -> 277 us (1.018)
  waiting for transfers between devices: 189 us -> 199 us
  local copies, waits for them, and re-layouts: 15.8 us -> 12.9 us
    reduce_scatter x0 -> x1, waiting for transfers between devices: none -> 46.1 us  [body(): lax.psum_scatter(placed, ('y', 'c'), scatter_dimension=0, tiled=True)[0]]
    all_gather x1 -> x0, waiting for transfers between devices: 33.6 us -> none  [body(): gathered = lax.all_gather(gathered, ('y', 'c'), axis=0, tiled=True)]
    reshape x3 -> x2, local copies, waits for them, and re-layouts: 3.84 us -> 0.42 us  [the longest x1 0.33 us: body(): lax.all_gather(panel[0], 'zh', axis=0, tiled=True)]
    all_gather x1, waiting for transfers between devices: 94.6 us -> 91.7 us  [body(): lax.all_gather(lax.all_gather(picked, 'x', axis=1, tiled=True), 'zl', axi...]
    all_gather x1, local copies, waits for them, and re-layouts: 3.06 us -> 0.22 us  [body(): lax.all_gather(panel[0], 'zh', axis=0, tiled=True)]
  transfers between devices with their start and end apart: 4 -> 4, of which waited for: 4 -> 4; matrix products, arithmetic and copies ran while one was open for 2% -> 1% of each run, Pallas kernels for 0% -> 0%
where the time goes in v6:
time: 277 us
  waiting for transfers between devices  199 us (72%)
  blocking collectives  28.7 us (10%)
  between operations  13.2 us (5%)
  local copies, waits for them, and re-layouts  12.9 us (5%)
  starting transfers between devices  11.9 us (4%)
  matrix products  6.67 us (2%)
  other arithmetic  4.91 us (2%)
    all_gather x1, waiting for transfers between devices, body(): lax.all_gather(lax.all_gather(picked, 'x', axis=1, tiled=True), 'zl', axi...  91.7 us
    reduce_scatter x1, waiting for transfers between devices, body(): lax.psum_scatter(placed, ('y', 'c'), scatter_dimension=0, tiled=True)[0]  46.1 us
    reduce_scatter x1, waiting for transfers between devices, body(): lax.psum_scatter(partial_value, ('y', 'c'), scatter_dimension=0, tiled=True)  39.2 us
    ppermute x1, waiting for transfers between devices, body(): summed = mine + lax.ppermute(other, 'zh', [(0, 1), (1, 0)])  21.7 us
    all_gather x1, blocking collectives, body(): lax.all_gather(panel[0], 'zh', axis=0, tiled=True)  17 us
    ppermute x1, starting transfers between devices, body(): summed = mine + lax.ppermute(other, 'zh', [(0, 1), (1, 0)])  11.8 us
    all_gather x1, blocking collectives, body(): lax.all_gather(picked, 'x', axis=1, tiled=True)  11.7 us
    dot_general x1, matrix products, body(): jnp.einsum('mk,kyzcn->yczmn', anc_kept, rhs, preferred_element_type=jnp.f...  6.3 us
  transfers between devices with their start and end apart: 4, of which 4 were waited for; matrix products, arithmetic and copies ran while one was open for 1% of the time, Pallas kernels for 0%

profile of v6, /device:TPU:25, one launch (start us, length us, event | category | flops | bytes accessed | tf_op | source)
XLA Modules:
  0.0 277.1 jit_solution(7155069866803910740)
XLA Ops:
  6.5 0.0 reduce-scatter.3.cloned.1.call-start
  6.5 0.5 broadcast.253
  7.1 1.3 subtract_bitcast_fusion
  8.4 0.1 reshape_squeeze.6
  8.5 0.1 reshape.278
  8.6 0.8 convert_reduce_fusion
  9.5 0.1 iota_add_fusion
  9.5 0.1 add.120
  9.6 0.1 broadcast_compare_fusion
  9.7 17.0 %all-gather = bf16[1,1536,64]{1,2,0:T(8,128)(2,1)S(1)} all-gather(bf16[1,768,64]{1,2,0:T(8,128)(2,1)} %param.4), channel_id=2, replica_groups=mesh['zl'=8,'x'=4,'y'=4,'zh'=2,'c'=2] {'zh'}, dimensions={1}, use_global_device_ids=true | all-gather | bytes 294912 | tf_op jit(solution)/shard_map/all_gather | solution.py:26
  26.7 0.0 copy-start
  26.7 0.2 copy.26
  26.9 0.3 reshape.294
  27.2 0.4 convolution_convert_fusion
  27.6 1.5 copy.27
  29.1 0.0 reduce-scatter.3.cloned.1.call-update
  29.1 0.0 all-gather.3.cloned.1.call-start
  29.2 46.1 %reduce-scatter.3.cloned.1.call-done = bf16[1,7,8192]{2,1,0:T(8,128)(2,1)} async-done(((bf16[8,7,8192]{2,1,0:T(8,128)(2,1)}), bf16[1,7,8192]{2,1,0:T(8,128)(2,1)}) %reduce-scatter.3.cloned.1.call-update) | async-done | bytes 114704 | tf_op jit(solution)/shard_map/reduce_scatter | solution.py:41
  75.3 1.1 reshape_squeeze.7
  76.5 0.1 copy.28
  76.6 11.7 %all_gather.10 = bf16[896,256]{0,1:T(8,128)(2,1)} all-gather(bf16[896,64]{0,1:T(8,128)(2,1)S(1)} %copy.28), channel_id=1, replica_groups=mesh['zl'=8,'x'=4,'y'=4,'zh'=2,'c'=2] {'x'}, dimensions={1}, use_global_device_ids=true | all-gather | bytes 573440 | tf_op jit(solution)/shard_map/all_gather | solution.py:50
  88.3 0.0 all-gather.3.cloned.1.call-update
  88.3 0.0 reduce-scatter.5.cloned.1.call-start
  88.4 0.1 fusion.6
  88.5 0.2 reduce-window.8
  88.7 0.0 copy-done
  88.7 0.5 copy.29
  89.2 0.7 copy.30
  89.9 0.1 select_reduce_fusion
  90.0 0.7 gather_fusion
  90.8 0.2 select_bitcast_fusion
  90.9 0.5 copy.31
  91.5 91.7 %all-gather.3.cloned.1.call-done = bf16[896,2048]{0,1:T(8,128)(2,1)} async-done(((bf16[896,256]{0,1:T(8,128)(2,1)}), bf16[896,2048]{0,1:T(8,128)(2,1)}) %all-gather.3.cloned.1.call-update) | async-done | bytes 3670032 | tf_op jit(solution)/shard_map/all_gather | solution.py:50
  183.2 6.3 %convolution_bitcast_fusion = f32[4,2,2,512,128]{3,4,1,2,0:T(8,128)} fusion(bf16[896,4,2,2,128]{0,4,3,2,1:T(8,128)(2,1)} %bitcast.45, bf16[512,896,1,1,1]{0,1,4,3,2:T(8,128)(2,1)S(1)} %bitcast.42), kind=kOutput, calls=%fused_computation.2 | convolution fusion | flops 1879048192 | bytes 8781824 | tf_op jit(solution)/shard_map/mk,kyzcn->yczmn/dot_general | solution.py:54
  189.5 5.2 %copy.33 = f32[4,2,2,512,128]{4,3,2,1,0:T(8,128)} copy(f32[4,2,2,512,128]{3,4,1,2,0:T(8,128)} %convolution_bitcast_fusion) | data formatting | bytes 8388608 | tf_op jit(solution)/shard_map/mk,kyzcn->yczmn/transpose | solution.py:54
  194.7 0.0 copy-start.1
  194.7 0.0 reduce-scatter.5.cloned.1.call-update
  194.8 39.2 %reduce-scatter.5.cloned.1.call-done = f32[1,2,512,128]{3,2,1,0:T(8,128)} async-done(((f32[8,2,512,128]{3,2,1,0:T(8,128)}), f32[1,2,512,128]{3,2,1,0:T(8,128)}) %reduce-scatter.5.cloned.1.call-update) | async-done | bytes 524304 | tf_op jit(solution)/shard_map/reduce_scatter | solution.py:56
  234.0 1.0 dynamic-slice_bitcast_fusion
  235.0 11.8 %collective-permute-start = (f32[512,128]{1,0:T(8,128)S(1)}, f32[512,128]{1,0:T(8,128)S(1)}, u32[]{:S(2)}, u32[]{:S(2)}) collective-permute-start(f32[512,128]{1,0:T(8,128)S(1)} %dynamic-slice_bitcast_fusion), channel_id=1, source_target_pairs={{0,2},{2,0},{1,3},{3,1},{4,6},{6,4},{5,7},{7,5},{8,10},{10,8},{9,1... | collective-permute-start | bytes 786440 | tf_op jit(solution)/shard_map/ppermute | solution.py:59
  246.8 0.0 copy-done.1
  246.8 0.2 compare_reduce_fusion
  247.0 0.1 broadcast_bitcast_fusion
  247.1 21.7 %collective-permute-done = f32[512,128]{1,0:T(8,128)S(1)} collective-permute-done((f32[512,128]{1,0:T(8,128)S(1)}, f32[512,128]{1,0:T(8,128)S(1)}, u32[]{:S(2)}, u32[]{:S(2)}) %collective-permute-start) | collective-permute-done | bytes 262176 | tf_op jit(solution)/shard_map/ppermute | solution.py:59
  268.7 1.8 fusion.2
  (10 shorter events, 0.1 us)
Async XLA Ops:
  6.5 68.8 %reduce-scatter.3.cloned.1.call-start = ((), (), s32[]{:S(2)}) async-start(), calls=%async_computation.2 | async-start | bytes 1179648 | tf_op jit(solution)/shard_map/reduce_scatter | solution.py:41
  26.7 62.0 %copy-start = (bf16[512,1024]{1,0:T(8,128)(2,1)S(1)}, bf16[512,1024]{1,0:T(8,128)(2,1)}, u32[]{:S(2)}) copy-start(bf16[512,1024]{1,0:T(8,128)(2,1)} %param.3) | copy-start | bytes 3145732
  29.1 154.1 %all-gather.3.cloned.1.call-start = ((), (), s32[]{:S(2)}) async-start(), calls=%async_computation.3 | async-start | bytes 4128768 | tf_op jit(solution)/shard_map/all_gather | solution.py:50
  88.3 145.7 %reduce-scatter.5.cloned.1.call-start = ((), (), s32[]{:S(2)}) async-start(), calls=%async_computation.4 | async-start | bytes 4718592 | tf_op jit(solution)/shard_map/reduce_scatter | solution.py:56
  194.7 52.0 %copy-start.1 = (s32[1,96]{1,0:T(1,128)S(1)}, s32[1,96]{1,0:T(1,128)}, u32[]{:S(2)}) copy-start(s32[1,96]{1,0:T(1,128)} %param.5) | copy-start | bytes 1156
  235.0 33.8 %collective-permute-start = (f32[512,128]{1,0:T(8,128)S(1)}, f32[512,128]{1,0:T(8,128)S(1)}, u32[]{:S(2)}, u32[]{:S(2)}) collective-permute-start(f32[512,128]{1,0:T(8,128)S(1)} %dynamic-slice_bitcast_fusion), channel_id=1, source_target_pairs={{0,2},{2,0},{1,3},{3,1},{4,6},{6,4},{5,7},{7,5},{8,10},{10,8},{9,1... | collective-permute-start | bytes 786440 | tf_op jit(solution)/shard_map/ppermute | solution.py:59
Sparse Core Ops, SparseCore 0:
  29.3 45.9 reduce-scatter.2
  88.4 94.7 all-gather.2
  194.9 39.0 reduce-scatter.4

commit v7 on v3

--- a/solution.py
+++ b/solution.py
@@ -19,13 +19,15 @@
     group_blocks = local_cols // BS
     local_width = panel.shape[2]
     per_dev = panel.shape[1] // BS
-    gathered = lax.all_gather(panel[0], "zh", axis=0, tiled=True)
+    lanes = BS
+    dense = panel[0].reshape(-1, lanes)
+    gathered = lax.all_gather(dense, "zh", axis=0, tiled=True)
     gathered = lax.all_gather(gathered, ("y", "c"), axis=0, tiled=True)
     blocks_of = structure[0]
     blocks_gathered = blocks_of.reshape(n_y, n_zh, n_c, per_dev).transpose(0, 2, 1, 3).reshape(SBLK)
     own_blocks = row_index * (local_rows // BS) + jnp.arange(local_rows // BS, dtype=jnp.int32)
     block_ids = jnp.arange(group_blocks, dtype=jnp.int32)
-    compact = gathered.reshape(SBLK, BS * local_width)
+    compact = gathered.reshape(SBLK, -1, lanes)
     local_block = blocks_gathered - col_index * group_blocks
     hits = local_block[None, :] == block_ids[:, None]
     present = jnp.any(hits, axis=1)
@@ -35,7 +37,7 @@
     picker = jnp.dot(slot_of.astype(jnp.float32), hits.astype(jnp.float32)).astype(jnp.bfloat16)
     slot_block = jnp.sum(jnp.where(slot_of, block_ids[None, :], 0), axis=1)
     picked = (
-        jnp.dot(picker, compact, preferred_element_type=jnp.float32)
+        jnp.einsum("jp,prl->jrl", picker, compact, preferred_element_type=jnp.float32)
         .astype(jnp.bfloat16)
         .reshape(CAP * BS, local_width)
     )

time: 272 us -> 268 us (0.985)
  local copies, waits for them, and re-layouts: 15.8 us -> 10.5 us
  waiting for transfers between devices: 189 us -> 193 us
    reshape x3 -> x2, local copies, waits for them, and re-layouts: 3.84 us -> 0.27 us  [body(): picked = jnp.einsum('jp,prl->jrl', picker, compact, preferred_element_typ...]
    all_gather x1, waiting for transfers between devices: 33.6 us -> 37.2 us  [body(): gathered = lax.all_gather(gathered, ('y', 'c'), axis=0, tiled=True)]
    all_gather x1 -> x0, local copies, waits for them, and re-layouts: 3.06 us -> none  [body(): gathered = lax.all_gather(gathered, ('y', 'c'), axis=0, tiled=True)]
where the time goes in v7:
time: 268 us
  waiting for transfers between devices  193 us (72%)
  blocking collectives  27.8 us (10%)
  between operations  13.3 us (5%)
  starting transfers between devices  11.9 us (4%)
  local copies, waits for them, and re-layouts  10.5 us (4%)
  matrix products  8.65 us (3%)
  other arithmetic  3.26 us (1%)
    all_gather x1, waiting for transfers between devices, body(): lax.all_gather(lax.all_gather(picked, 'x', axis=1, tiled=True), 'zl', axi...  94.6 us
    reduce_scatter x1, waiting for transfers between devices, body(): lax.psum_scatter(partial_value, ('y', 'c'), scatter_dimension=0, tiled=True)  39.2 us
    all_gather x1, waiting for transfers between devices, body(): gathered = lax.all_gather(gathered, ('y', 'c'), axis=0, tiled=True)  37.2 us
    ppermute x1, waiting for transfers between devices, body(): summed = mine + lax.ppermute(other, 'zh', [(0, 1), (1, 0)])  21.6 us
    all_gather x1, blocking collectives, body(): gathered = lax.all_gather(dense, 'zh', axis=0, tiled=True)  16.8 us
    ppermute x1, starting transfers between devices, body(): summed = mine + lax.ppermute(other, 'zh', [(0, 1), (1, 0)])  11.8 us
    all_gather x1, blocking collectives, body(): lax.all_gather(picked, 'x', axis=1, tiled=True)  11 us
    dot_general x1, matrix products, body(): jnp.einsum('mk,kyzcn->yczmn', anc_kept, rhs, preferred_element_type=jnp.f...  6.3 us
  transfers between devices with their start and end apart: 4, of which 4 were waited for; matrix products, arithmetic and copies ran while one was open for 2% of the time, Pallas kernels for 0%

profile of v7, /device:TPU:25, one launch (start us, length us, event | category | flops | bytes accessed | tf_op | source)
XLA Modules:
  0.0 268.0 jit_solution(3737916558864031067)
XLA Ops:
  6.5 0.0 copy-start
  6.5 0.0 all-gather.3.cloned.1.call-start
  6.5 1.1 copy.34
  7.7 0.1 reshape_squeeze.4
  7.8 16.8 %all_gather.12 = bf16[768,128]{1,0:T(8,128)(2,1)} all-gather(bf16[384,128]{1,0:T(8,128)(2,1)S(1)} %reshape_squeeze.4), channel_id=1, replica_groups=mesh['zl'=8,'x'=4,'y'=4,'zh'=2,'c'=2] {'zh'}, dimensions={0}, use_global_device_ids=true | all-gather | bytes 294912 | tf_op jit(solution)/shard_map/all_gather | solution.py:24
  24.6 0.0 all-gather.3.cloned.1.call-update
  24.7 0.0 all-gather.5.cloned.1.call-start
  24.7 0.7 subtract_reduce_fusion
  25.4 0.1 sub.29
  25.5 0.1 sub.31
  25.6 0.1 fusion.9
  25.7 0.2 reduce-window.8
  25.9 37.2 %all-gather.3.cloned.1.call-done = bf16[6144,128]{1,0:T(8,128)(2,1)} async-done(((bf16[768,128]{1,0:T(8,128)(2,1)}), bf16[6144,128]{1,0:T(8,128)(2,1)}) %all-gather.3.cloned.1.call-update) | async-done | bytes 1572880 | tf_op jit(solution)/shard_map/all_gather | solution.py:25
  63.1 2.3 fusion.2
  65.5 0.1 reshape.119
  65.6 0.1 copy.37
  65.7 11.0 %all_gather.14 = bf16[896,256]{0,1:T(8,128)(2,1)} all-gather(bf16[896,64]{0,1:T(8,128)(2,1)S(1)} %copy.37), channel_id=1, replica_groups=mesh['zl'=8,'x'=4,'y'=4,'zh'=2,'c'=2] {'x'}, dimensions={1}, use_global_device_ids=true | all-gather | bytes 573440 | tf_op jit(solution)/shard_map/all_gather | solution.py:45
  76.7 0.0 all-gather.5.cloned.1.call-update
  76.7 0.0 reduce-scatter.2.cloned.1.call-start
  76.8 0.0 copy-done
  76.8 0.5 copy.38
  77.3 0.7 copy.39
  78.0 0.1 select_reduce_fusion
  78.1 0.7 gather_fusion
  78.9 0.2 select_bitcast_fusion
  79.0 0.5 copy.40
  79.6 94.6 %all-gather.5.cloned.1.call-done = bf16[896,2048]{0,1:T(8,128)(2,1)} async-done(((bf16[896,256]{0,1:T(8,128)(2,1)}), bf16[896,2048]{0,1:T(8,128)(2,1)}) %all-gather.5.cloned.1.call-update) | async-done | bytes 3670032 | tf_op jit(solution)/shard_map/all_gather | solution.py:45
  174.2 6.3 %convolution_bitcast_fusion = f32[4,2,2,512,128]{3,4,1,2,0:T(8,128)} fusion(bf16[896,4,2,2,128]{0,4,3,2,1:T(8,128)(2,1)} %bitcast.46, bf16[512,896,1,1,1]{0,1,4,3,2:T(8,128)(2,1)S(1)} %bitcast.44), kind=kOutput, calls=%fused_computation.1 | convolution fusion | flops 1879048192 | bytes 8781824 | tf_op jit(solution)/shard_map/mk,kyzcn->yczmn/dot_general | solution.py:49
  180.5 5.2 %copy.42 = f32[4,2,2,512,128]{4,3,2,1,0:T(8,128)} copy(f32[4,2,2,512,128]{3,4,1,2,0:T(8,128)} %convolution_bitcast_fusion) | data formatting | bytes 8388608 | tf_op jit(solution)/shard_map/mk,kyzcn->yczmn/transpose | solution.py:49
  185.7 0.0 copy-start.1
  185.7 0.0 reduce-scatter.2.cloned.1.call-update
  185.8 39.2 %reduce-scatter.2.cloned.1.call-done = f32[1,2,512,128]{3,2,1,0:T(8,128)} async-done(((f32[8,2,512,128]{3,2,1,0:T(8,128)}), f32[1,2,512,128]{3,2,1,0:T(8,128)}) %reduce-scatter.2.cloned.1.call-update) | async-done | bytes 524304 | tf_op jit(solution)/shard_map/reduce_scatter | solution.py:51
  225.0 1.0 dynamic-slice_bitcast_fusion
  225.9 11.8 %collective-permute-start = (f32[512,128]{1,0:T(8,128)S(1)}, f32[512,128]{1,0:T(8,128)S(1)}, u32[]{:S(2)}, u32[]{:S(2)}) collective-permute-start(f32[512,128]{1,0:T(8,128)S(1)} %dynamic-slice_bitcast_fusion), channel_id=1, source_target_pairs={{0,2},{2,0},{1,3},{3,1},{4,6},{6,4},{5,7},{7,5},{8,10},{10,8},{9,1... | collective-permute-start | bytes 786440 | tf_op jit(solution)/shard_map/ppermute | solution.py:54
  237.8 0.0 copy-done.1
  237.8 0.2 compare_reduce_fusion
  238.0 0.1 broadcast_bitcast_fusion
  238.1 21.6 %collective-permute-done = f32[512,128]{1,0:T(8,128)S(1)} collective-permute-done((f32[512,128]{1,0:T(8,128)S(1)}, f32[512,128]{1,0:T(8,128)S(1)}, u32[]{:S(2)}, u32[]{:S(2)}) %collective-permute-start) | collective-permute-done | bytes 262176 | tf_op jit(solution)/shard_map/ppermute | solution.py:54
  259.7 1.8 fusion.8
  (8 shorter events, 0.1 us)
Async XLA Ops:
  6.5 70.2 %copy-start = (bf16[512,1024]{1,0:T(8,128)(2,1)S(1)}, bf16[512,1024]{1,0:T(8,128)(2,1)}, u32[]{:S(2)}) copy-start(bf16[512,1024]{1,0:T(8,128)(2,1)} %param.3) | copy-start | bytes 3145732
  6.5 56.5 %all-gather.3.cloned.1.call-start = ((), (), s32[]{:S(2)}) async-start(), calls=%async_computation.1 | async-start | bytes 1769472 | tf_op jit(solution)/shard_map/all_gather | solution.py:25
  24.7 149.5 %all-gather.5.cloned.1.call-start = ((), (), s32[]{:S(2)}) async-start(), calls=%async_computation.2 | async-start | bytes 4128768 | tf_op jit(solution)/shard_map/all_gather | solution.py:45
  76.7 148.3 %reduce-scatter.2.cloned.1.call-start = ((), (), s32[]{:S(2)}) async-start(), calls=%async_computation.3 | async-start | bytes 4718592 | tf_op jit(solution)/shard_map/reduce_scatter | solution.py:51
  185.7 52.1 %copy-start.1 = (s32[1,96]{1,0:T(1,128)S(1)}, s32[1,96]{1,0:T(1,128)}, u32[]{:S(2)}) copy-start(s32[1,96]{1,0:T(1,128)} %param.5) | copy-start | bytes 1156
  225.9 33.7 %collective-permute-start = (f32[512,128]{1,0:T(8,128)S(1)}, f32[512,128]{1,0:T(8,128)S(1)}, u32[]{:S(2)}, u32[]{:S(2)}) collective-permute-start(f32[512,128]{1,0:T(8,128)S(1)} %dynamic-slice_bitcast_fusion), channel_id=1, source_target_pairs={{0,2},{2,0},{1,3},{3,1},{4,6},{6,4},{5,7},{7,5},{8,10},{10,8},{9,1... | collective-permute-start | bytes 786440 | tf_op jit(solution)/shard_map/ppermute | solution.py:54
Sparse Core Ops, SparseCore 0:
  24.8 38.2 all-gather.2
  76.8 97.3 all-gather.4
  185.9 39.0 reduce-scatter.1

commit v8 on v7

--- a/solution.py
+++ b/solution.py
@@ -21,26 +21,32 @@
     per_dev = panel.shape[1] // BS
     lanes = BS
     dense = panel[0].reshape(-1, lanes)
-    gathered = lax.all_gather(dense, "zh", axis=0, tiled=True)
-    gathered = lax.all_gather(gathered, ("y", "c"), axis=0, tiled=True)
+    gathered = lax.all_gather(dense, ("y", "c"), axis=0, tiled=True)
     blocks_of = structure[0]
-    blocks_gathered = blocks_of.reshape(n_y, n_zh, n_c, per_dev).transpose(0, 2, 1, 3).reshape(SBLK)
+    by_col = blocks_of.reshape(n_y, n_zh, n_c, per_dev)
+    blocks_half = lax.dynamic_index_in_dim(by_col, zh_index, 1, False).reshape(-1)
     own_blocks = row_index * (local_rows // BS) + jnp.arange(local_rows // BS, dtype=jnp.int32)
     block_ids = jnp.arange(group_blocks, dtype=jnp.int32)
-    compact = gathered.reshape(SBLK, -1, lanes)
-    local_block = blocks_gathered - col_index * group_blocks
+    compact = gathered.reshape(blocks_half.shape[0], -1, lanes)
+    same_group = (blocks_half[:, None] // group_blocks) == (blocks_of[None, :] // group_blocks)
+    slot = jnp.sum(same_group & (blocks_of[None, :] < blocks_half[:, None]), axis=1)
+    slot_ids = jnp.arange(CAP, dtype=jnp.int32)
+    partner_col = col_index + (1 - 2 * zh_index) * n_c
+
+    def pick(group):
+        chosen = ((blocks_half // group_blocks)[None, :] == group) & (slot[None, :] == slot_ids[:, None])
+        return jnp.einsum(
+            "jp,prl->jrl", chosen.astype(jnp.bfloat16), compact, preferred_element_type=jnp.float32
+        ).astype(jnp.bfloat16)
+
+    from_partner = lax.ppermute(pick(partner_col), "zh", [(0, 1), (1, 0)])
+    picked = (pick(col_index) + from_partner).reshape(CAP * BS, local_width)
+    local_block = blocks_of - col_index * group_blocks
     hits = local_block[None, :] == block_ids[:, None]
     present = jnp.any(hits, axis=1)
     rank = jnp.cumsum(present.astype(jnp.int32)) - 1
-    slot_ids = jnp.arange(CAP, dtype=jnp.int32)
     slot_of = present[None, :] & (rank[None, :] == slot_ids[:, None])
-    picker = jnp.dot(slot_of.astype(jnp.float32), hits.astype(jnp.float32)).astype(jnp.bfloat16)
     slot_block = jnp.sum(jnp.where(slot_of, block_ids[None, :], 0), axis=1)
-    picked = (
-        jnp.einsum("jp,prl->jrl", picker, compact, preferred_element_type=jnp.float32)
-        .astype(jnp.bfloat16)
-        .reshape(CAP * BS, local_width)
-    )
     anc_kept = jnp.take(anc_inv.reshape(local_rows, group_blocks, BS), slot_block, axis=1).reshape(local_rows, CAP * BS)
     expanded = lax.all_gather(lax.all_gather(picked, "x", axis=1, tiled=True), "zl", axis=1, tiled=True)
     width = expanded.shape[1]

time: 268 us -> 256 us (0.955)
  waiting for transfers between devices: 193 us -> 166 us
  starting transfers between devices: 11.9 us -> 24.3 us
    all_gather x1 -> x0, waiting for transfers between devices: 37.2 us -> none  [body(): gathered = lax.all_gather(gathered, ('y', 'c'), axis=0, tiled=True)]
    ppermute x0 -> x1, starting transfers between devices: none -> 12.5 us  [body(): from_partner = lax.ppermute(pick(partner_col), 'zh', [(0, 1), (1, 0)])]
    all_gather x1, waiting for transfers between devices: 94.6 us -> 101 us  [body(): lax.all_gather(lax.all_gather(picked, 'x', axis=1, tiled=True), 'zl', axi...]
    ppermute x0 -> x1, waiting for transfers between devices: none -> 3.7 us  [body(): from_partner = lax.ppermute(pick(partner_col), 'zh', [(0, 1), (1, 0)])]
  transfers between devices with their start and end apart: 4 -> 4, of which waited for: 4 -> 4; matrix products, arithmetic and copies ran while one was open for 2% -> 1% of each run, Pallas kernels for 0% -> 0%
where the time goes in v8:
time: 256 us; the launch traced here: 255 us
  waiting for transfers between devices  166 us (65%)
  blocking collectives  29 us (11%)
  starting transfers between devices  24.3 us (9%)
  between operations  13.6 us (5%)
  local copies, waits for them, and re-layouts  10.9 us (4%)
  matrix products  7.36 us (3%)
  other arithmetic  4.75 us (2%)
    all_gather x1, waiting for transfers between devices, body(): lax.all_gather(lax.all_gather(picked, 'x', axis=1, tiled=True), 'zl', axi...  101 us
    reduce_scatter x1, waiting for transfers between devices, body(): lax.psum_scatter(partial_value, ('y', 'c'), scatter_dimension=0, tiled=True)  39.2 us
    ppermute x1, waiting for transfers between devices, body(): summed = mine + lax.ppermute(other, 'zh', [(0, 1), (1, 0)])  21.7 us
    all_gather x1, blocking collectives, body(): gathered = lax.all_gather(dense, ('y', 'c'), axis=0, tiled=True)  16.9 us
    ppermute x1, starting transfers between devices, body(): from_partner = lax.ppermute(pick(partner_col), 'zh', [(0, 1), (1, 0)])  12.5 us
    all_gather x1, blocking collectives, body(): lax.all_gather(picked, 'x', axis=1, tiled=True)  12.1 us
    ppermute x1, starting transfers between devices, body(): summed = mine + lax.ppermute(other, 'zh', [(0, 1), (1, 0)])  11.8 us
    dot_general x1, matrix products, body(): jnp.einsum('mk,kyzcn->yczmn', anc_kept, rhs, preferred_element_type=jnp.f...  6.3 us
  transfers between devices with their start and end apart: 4, of which 4 were waited for; matrix products, arithmetic and copies ran while one was open for 1% of the time, Pallas kernels for 0%

profile of v8, /device:TPU:25, one launch (start us, length us, event | category | flops | bytes accessed | tf_op | source)
XLA Modules:
  0.0 255.5 jit_solution(6091373954934968795)
XLA Ops:
  6.5 0.0 copy-start
  6.5 0.0 all-gather.2.cloned.1.call-start
  6.5 0.5 broadcast.212
  7.1 1.3 subtract_bitcast_fusion
  8.4 0.1 reshape_squeeze.6
  8.5 0.1 reshape.215
  8.6 1.1 copy.32
  9.7 0.1 reshape_squeeze.7
  9.8 16.9 %all_gather.9 = bf16[3072,128]{1,0:T(8,128)(2,1)S(1)} all-gather(bf16[384,128]{1,0:T(8,128)(2,1)S(1)} %reshape_squeeze.7), channel_id=1, replica_groups=mesh['zl'=8,'x'=4,'y'=4,'zh'=2,'c'=2] {'y','c'}, dimensions={0}, use_global_device_ids=true | all-gather | bytes 884736 | tf_op jit(solution)/shard_map/all_gather | solution.py:24
  26.8 0.8 convert_reduce_fusion
  27.6 0.5 convolution_convert_fusion
  28.1 12.5 %collective-permute-start = (bf16[7,64,128]{2,0,1:T(8,128)(2,1)S(1)}, bf16[7,64,128]{2,0,1:T(8,128)(2,1)S(1)}, u32[]{:S(2)}, u32[]{:S(2)}) collective-permute-start(bf16[7,64,128]{2,0,1:T(8,128)(2,1)S(1)} %convolution_convert_fusion), channel_id=1, source_target_pairs={{0,2},{2,0},{1,3},{3,1},{4,6},{6,4},{5,7},{7,5},{8,10},{10,8},{9,1... | collective-permute-start | bytes 344072 | tf_op jit(solution)/shard_map/ppermute | solution.py:42
  40.6 3.7 %collective-permute-done = bf16[7,64,128]{2,0,1:T(8,128)(2,1)S(1)} collective-permute-done((bf16[7,64,128]{2,0,1:T(8,128)(2,1)S(1)}, bf16[7,64,128]{2,0,1:T(8,128)(2,1)S(1)}, u32[]{:S(2)}, u32[]{:S(2)}) %collective-permute-start) | collective-permute-done | bytes 114720 | tf_op jit(solution)/shard_map/ppermute | solution.py:42
  44.3 0.5 fusion
  44.9 0.1 reshape.217
  45.0 0.1 copy.36
  45.2 12.1 %all_gather.10 = bf16[896,256]{0,1:T(8,128)(2,1)} all-gather(bf16[896,64]{0,1:T(8,128)(2,1)S(1)} %copy.36), channel_id=1, replica_groups=mesh['zl'=8,'x'=4,'y'=4,'zh'=2,'c'=2] {'x'}, dimensions={1}, use_global_device_ids=true | all-gather | bytes 573440 | tf_op jit(solution)/shard_map/all_gather | solution.py:51
  57.2 0.0 all-gather.2.cloned.1.call-update
  57.3 0.0 reduce-scatter.2.cloned.1.call-start
  57.3 0.1 fusion.12
  57.4 0.2 reduce-window.8
  57.6 0.0 copy-done
  57.6 0.5 copy.37
  58.2 0.7 copy.38
  58.9 0.1 select_reduce_fusion
  59.0 0.7 gather_fusion
  59.7 0.2 select_bitcast_fusion
  59.9 0.5 copy.39
  60.4 100.9 %all-gather.2.cloned.1.call-done = bf16[896,2048]{0,1:T(8,128)(2,1)} async-done(((bf16[896,256]{0,1:T(8,128)(2,1)}), bf16[896,2048]{0,1:T(8,128)(2,1)}) %all-gather.2.cloned.1.call-update) | async-done | bytes 3670032 | tf_op jit(solution)/shard_map/all_gather | solution.py:51
  161.3 6.3 %convolution_bitcast_fusion = f32[4,2,2,512,128]{3,4,1,2,0:T(8,128)} fusion(bf16[896,4,2,2,128]{0,4,3,2,1:T(8,128)(2,1)} %bitcast.53, bf16[512,896,1,1,1]{0,1,4,3,2:T(8,128)(2,1)S(1)} %bitcast.50), kind=kOutput, calls=%fused_computation.1 | convolution fusion | flops 1879048192 | bytes 8781824 | tf_op jit(solution)/shard_map/mk,kyzcn->yczmn/dot_general | solution.py:55
  167.6 5.2 %copy.41 = f32[4,2,2,512,128]{4,3,2,1,0:T(8,128)} copy(f32[4,2,2,512,128]{3,4,1,2,0:T(8,128)} %convolution_bitcast_fusion) | data formatting | bytes 8388608 | tf_op jit(solution)/shard_map/mk,kyzcn->yczmn/transpose | solution.py:55
  172.8 0.0 copy-start.1
  172.8 0.0 reduce-scatter.2.cloned.1.call-update
  172.9 39.2 %reduce-scatter.2.cloned.1.call-done = f32[1,2,512,128]{3,2,1,0:T(8,128)} async-done(((f32[8,2,512,128]{3,2,1,0:T(8,128)}), f32[1,2,512,128]{3,2,1,0:T(8,128)}) %reduce-scatter.2.cloned.1.call-update) | async-done | bytes 524304 | tf_op jit(solution)/shard_map/reduce_scatter | solution.py:57
  212.1 1.0 dynamic-slice_bitcast_fusion
  213.1 11.8 %collective-permute-start.1 = (f32[512,128]{1,0:T(8,128)S(1)}, f32[512,128]{1,0:T(8,128)S(1)}, u32[]{:S(2)}, u32[]{:S(2)}) collective-permute-start(f32[512,128]{1,0:T(8,128)S(1)} %dynamic-slice_bitcast_fusion), channel_id=1, source_target_pairs={{0,2},{2,0},{1,3},{3,1},{4,6},{6,4},{5,7},{7,5},{8,10},{10,8},{9,1... | collective-permute-start | bytes 786440 | tf_op jit(solution)/shard_map/ppermute | solution.py:60
  224.9 0.0 copy-done.1
  224.9 0.2 compare_reduce_fusion
  225.1 0.1 broadcast_bitcast_fusion
  225.2 21.7 %collective-permute-done.1 = f32[512,128]{1,0:T(8,128)S(1)} collective-permute-done((f32[512,128]{1,0:T(8,128)S(1)}, f32[512,128]{1,0:T(8,128)S(1)}, u32[]{:S(2)}, u32[]{:S(2)}) %collective-permute-start.1) | collective-permute-done | bytes 262176 | tf_op jit(solution)/shard_map/ppermute | solution.py:60
  246.8 1.8 fusion.5
  (10 shorter events, 0.1 us)
Async XLA Ops:
  6.5 51.1 %copy-start = (bf16[512,1024]{1,0:T(8,128)(2,1)S(1)}, bf16[512,1024]{1,0:T(8,128)(2,1)}, u32[]{:S(2)}) copy-start(bf16[512,1024]{1,0:T(8,128)(2,1)} %param.3) | copy-start | bytes 3145732
  6.5 154.8 %all-gather.2.cloned.1.call-start = ((), (), s32[]{:S(2)}) async-start(), calls=%async_computation.1 | async-start | bytes 4128768 | tf_op jit(solution)/shard_map/all_gather | solution.py:51
  28.1 16.2 %collective-permute-start = (bf16[7,64,128]{2,0,1:T(8,128)(2,1)S(1)}, bf16[7,64,128]{2,0,1:T(8,128)(2,1)S(1)}, u32[]{:S(2)}, u32[]{:S(2)}) collective-permute-start(bf16[7,64,128]{2,0,1:T(8,128)(2,1)S(1)} %convolution_convert_fusion), channel_id=1, source_target_pairs={{0,2},{2,0},{1,3},{3,1},{4,6},{6,4},{5,7},{7,5},{8,10},{10,8},{9,1... | collective-permute-start | bytes 344072 | tf_op jit(solution)/shard_map/ppermute | solution.py:42
  57.3 154.8 %reduce-scatter.2.cloned.1.call-start = ((), (), s32[]{:S(2)}) async-start(), calls=%async_computation.2 | async-start | bytes 4718592 | tf_op jit(solution)/shard_map/reduce_scatter | solution.py:57
  172.8 52.0 %copy-start.1 = (s32[1,96]{1,0:T(1,128)S(1)}, s32[1,96]{1,0:T(1,128)}, u32[]{:S(2)}) copy-start(s32[1,96]{1,0:T(1,128)} %param.5) | copy-start | bytes 1156
  213.1 33.8 %collective-permute-start.1 = (f32[512,128]{1,0:T(8,128)S(1)}, f32[512,128]{1,0:T(8,128)S(1)}, u32[]{:S(2)}, u32[]{:S(2)}) collective-permute-start(f32[512,128]{1,0:T(8,128)S(1)} %dynamic-slice_bitcast_fusion), channel_id=1, source_target_pairs={{0,2},{2,0},{1,3},{3,1},{4,6},{6,4},{5,7},{7,5},{8,10},{10,8},{9,1... | collective-permute-start | bytes 786440 | tf_op jit(solution)/shard_map/ppermute | solution.py:60
Sparse Core Ops, SparseCore 0:
  57.4 103.8 all-gather.1
  173.0 39.0 reduce-scatter.1

commit v9 on v8

--- a/solution.py
+++ b/solution.py
@@ -39,7 +39,8 @@
             "jp,prl->jrl", chosen.astype(jnp.bfloat16), compact, preferred_element_type=jnp.float32
         ).astype(jnp.bfloat16)
 
-    from_partner = lax.ppermute(pick(partner_col), "zh", [(0, 1), (1, 0)])
+    both = lax.all_gather(pick(partner_col), "zh", axis=0, tiled=False)
+    from_partner = lax.dynamic_index_in_dim(both, 1 - zh_index, 0, keepdims=False)
     picked = (pick(col_index) + from_partner).reshape(CAP * BS, local_width)
     local_block = blocks_of - col_index * group_blocks
     hits = local_block[None, :] == block_ids[:, None]

time: 256 us -> 253 us (0.988)
  blocking collectives: 29 us -> 43.6 us
  starting transfers between devices: 24.3 us -> 11.9 us
  waiting for transfers between devices: 166 us -> 160 us
    all_gather x0 -> x1, blocking collectives: none -> 14.6 us  [body(): both = lax.all_gather(pick(partner_col), 'zh', axis=0, tiled=False)]
    ppermute x1 -> x0, starting transfers between devices: 12.5 us -> none  [body(): from_partner = lax.ppermute(pick(partner_col), 'zh', [(0, 1), (1, 0)])]
    ppermute x1 -> x0, waiting for transfers between devices: 3.7 us -> none  [body(): from_partner = lax.ppermute(pick(partner_col), 'zh', [(0, 1), (1, 0)])]
  transfers between devices with their start and end apart: 4 -> 3, of which waited for: 4 -> 3; matrix products, arithmetic and copies ran while one was open for 1% -> 1% of each run, Pallas kernels for 0% -> 0%
where the time goes in v9:
time: 253 us; the launch traced here: 252 us
  waiting for transfers between devices  160 us (63%)
  blocking collectives  43.6 us (17%)
  between operations  13.6 us (5%)
  starting transfers between devices  11.9 us (5%)
  local copies, waits for them, and re-layouts  10.9 us (4%)
  matrix products  7.36 us (3%)
  other arithmetic  4.75 us (2%)
    all_gather x1, waiting for transfers between devices, body(): lax.all_gather(lax.all_gather(picked, 'x', axis=1, tiled=True), 'zl', axi...  99.3 us
    reduce_scatter x1, waiting for transfers between devices, body(): lax.psum_scatter(partial_value, ('y', 'c'), scatter_dimension=0, tiled=True)  39.2 us
    ppermute x1, waiting for transfers between devices, body(): summed = mine + lax.ppermute(other, 'zh', [(0, 1), (1, 0)])  21.6 us
    all_gather x1, blocking collectives, body(): gathered = lax.all_gather(dense, ('y', 'c'), axis=0, tiled=True)  16.9 us
    all_gather x1, blocking collectives, body(): both = lax.all_gather(pick(partner_col), 'zh', axis=0, tiled=False)  14.6 us
    all_gather x1, blocking collectives, body(): lax.all_gather(picked, 'x', axis=1, tiled=True)  12.1 us
    ppermute x1, starting transfers between devices, body(): summed = mine + lax.ppermute(other, 'zh', [(0, 1), (1, 0)])  11.8 us
    dot_general x1, matrix products, body(): jnp.einsum('mk,kyzcn->yczmn', anc_kept, rhs, preferred_element_type=jnp.f...  6.3 us
  transfers between devices with their start and end apart: 3, of which 3 were waited for; matrix products, arithmetic and copies ran while one was open for 1% of the time, Pallas kernels for 0%

profile of v9, /device:TPU:25, one launch (start us, length us, event | category | flops | bytes accessed | tf_op | source)
XLA Modules:
  0.0 252.2 jit_solution(15339256059663943600)
XLA Ops:
  6.5 0.0 copy-start
  6.5 0.0 all-gather.3.cloned.1.call-start
  6.5 0.5 broadcast.212
  7.1 1.3 subtract_bitcast_fusion
  8.4 0.1 reshape_squeeze.6
  8.5 0.1 reshape.215
  8.6 1.1 copy.39
  9.6 0.1 reshape_squeeze.7
  9.8 16.9 %all_gather.15 = bf16[3072,128]{1,0:T(8,128)(2,1)S(1)} all-gather(bf16[384,128]{1,0:T(8,128)(2,1)S(1)} %reshape_squeeze.7), channel_id=1, replica_groups=mesh['zl'=8,'x'=4,'y'=4,'zh'=2,'c'=2] {'y','c'}, dimensions={0}, use_global_device_ids=true | all-gather | bytes 884736 | tf_op jit(solution)/shard_map/all_gather | solution.py:24
  26.7 0.8 convert_reduce_fusion
  27.6 0.5 convolution_convert_fusion
  28.1 14.6 %all-gather = bf16[14,64,128]{2,1,0:T(8,128)(2,1)S(1)} all-gather(bf16[7,64,128]{2,1,0:T(8,128)(2,1)S(1)} %copy.42), channel_id=2, replica_groups=mesh['zl'=8,'x'=4,'y'=4,'zh'=2,'c'=2] {'zh'}, dimensions={0}, use_global_device_ids=true | all-gather | bytes 344064 | tf_op jit(solution)/shard_map/all_gather | solution.py:42
  42.7 0.5 fusion
  43.3 0.1 reshape.217
  43.4 0.1 copy.45
  43.6 12.1 %all_gather.18 = bf16[896,256]{0,1:T(8,128)(2,1)} all-gather(bf16[896,64]{0,1:T(8,128)(2,1)S(1)} %copy.45), channel_id=1, replica_groups=mesh['zl'=8,'x'=4,'y'=4,'zh'=2,'c'=2] {'x'}, dimensions={1}, use_global_device_ids=true | all-gather | bytes 573440 | tf_op jit(solution)/shard_map/all_gather | solution.py:52
  55.7 0.0 all-gather.3.cloned.1.call-update
  55.7 0.0 reduce-scatter.2.cloned.1.call-start
  55.8 0.1 fusion.12
  55.9 0.2 reduce-window.8
  56.1 0.0 copy-done
  56.1 0.5 copy.46
  56.6 0.7 copy.47
  57.3 0.1 select_reduce_fusion
  57.4 0.7 gather_fusion
  58.2 0.2 select_bitcast_fusion
  58.3 0.5 copy.48
  58.9 99.3 %all-gather.3.cloned.1.call-done = bf16[896,2048]{0,1:T(8,128)(2,1)} async-done(((bf16[896,256]{0,1:T(8,128)(2,1)}), bf16[896,2048]{0,1:T(8,128)(2,1)}) %all-gather.3.cloned.1.call-update) | async-done | bytes 3670032 | tf_op jit(solution)/shard_map/all_gather | solution.py:52
  158.1 6.3 %convolution_bitcast_fusion = f32[4,2,2,512,128]{3,4,1,2,0:T(8,128)} fusion(bf16[896,4,2,2,128]{0,4,3,2,1:T(8,128)(2,1)} %bitcast.57, bf16[512,896,1,1,1]{0,1,4,3,2:T(8,128)(2,1)S(1)} %bitcast.53), kind=kOutput, calls=%fused_computation.1 | convolution fusion | flops 1879048192 | bytes 8781824 | tf_op jit(solution)/shard_map/mk,kyzcn->yczmn/dot_general | solution.py:56
  164.4 5.2 %copy.50 = f32[4,2,2,512,128]{4,3,2,1,0:T(8,128)} copy(f32[4,2,2,512,128]{3,4,1,2,0:T(8,128)} %convolution_bitcast_fusion) | data formatting | bytes 8388608 | tf_op jit(solution)/shard_map/mk,kyzcn->yczmn/transpose | solution.py:56
  169.6 0.0 copy-start.1
  169.6 0.0 reduce-scatter.2.cloned.1.call-update
  169.7 39.2 %reduce-scatter.2.cloned.1.call-done = f32[1,2,512,128]{3,2,1,0:T(8,128)} async-done(((f32[8,2,512,128]{3,2,1,0:T(8,128)}), f32[1,2,512,128]{3,2,1,0:T(8,128)}) %reduce-scatter.2.cloned.1.call-update) | async-done | bytes 524304 | tf_op jit(solution)/shard_map/reduce_scatter | solution.py:58
  208.9 1.0 dynamic-slice_bitcast_fusion
  209.9 11.8 %collective-permute-start = (f32[512,128]{1,0:T(8,128)S(1)}, f32[512,128]{1,0:T(8,128)S(1)}, u32[]{:S(2)}, u32[]{:S(2)}) collective-permute-start(f32[512,128]{1,0:T(8,128)S(1)} %dynamic-slice_bitcast_fusion), channel_id=1, source_target_pairs={{0,2},{2,0},{1,3},{3,1},{4,6},{6,4},{5,7},{7,5},{8,10},{10,8},{9,1... | collective-permute-start | bytes 786440 | tf_op jit(solution)/shard_map/ppermute | solution.py:61
  221.7 0.0 copy-done.1
  221.7 0.2 compare_reduce_fusion
  221.9 0.1 broadcast_bitcast_fusion
  222.0 21.6 %collective-permute-done = f32[512,128]{1,0:T(8,128)S(1)} collective-permute-done((f32[512,128]{1,0:T(8,128)S(1)}, f32[512,128]{1,0:T(8,128)S(1)}, u32[]{:S(2)}, u32[]{:S(2)}) %collective-permute-start) | collective-permute-done | bytes 262176 | tf_op jit(solution)/shard_map/ppermute | solution.py:61
  243.6 1.8 fusion.5
  (12 shorter events, 0.1 us)
Async XLA Ops:
  6.5 49.5 %copy-start = (bf16[512,1024]{1,0:T(8,128)(2,1)S(1)}, bf16[512,1024]{1,0:T(8,128)(2,1)}, u32[]{:S(2)}) copy-start(bf16[512,1024]{1,0:T(8,128)(2,1)} %param.3) | copy-start | bytes 3145732
  6.5 151.6 %all-gather.3.cloned.1.call-start = ((), (), s32[]{:S(2)}) async-start(), calls=%async_computation.1 | async-start | bytes 4128768 | tf_op jit(solution)/shard_map/all_gather | solution.py:52
  55.7 153.2 %reduce-scatter.2.cloned.1.call-start = ((), (), s32[]{:S(2)}) async-start(), calls=%async_computation.2 | async-start | bytes 4718592 | tf_op jit(solution)/shard_map/reduce_scatter | solution.py:58
  169.6 52.1 %copy-start.1 = (s32[1,96]{1,0:T(1,128)S(1)}, s32[1,96]{1,0:T(1,128)}, u32[]{:S(2)}) copy-start(s32[1,96]{1,0:T(1,128)} %param.5) | copy-start | bytes 1156
  209.9 33.7 %collective-permute-start = (f32[512,128]{1,0:T(8,128)S(1)}, f32[512,128]{1,0:T(8,128)S(1)}, u32[]{:S(2)}, u32[]{:S(2)}) collective-permute-start(f32[512,128]{1,0:T(8,128)S(1)} %dynamic-slice_bitcast_fusion), channel_id=1, source_target_pairs={{0,2},{2,0},{1,3},{3,1},{4,6},{6,4},{5,7},{7,5},{8,10},{10,8},{9,1... | collective-permute-start | bytes 786440 | tf_op jit(solution)/shard_map/ppermute | solution.py:61
Sparse Core Ops, SparseCore 0:
  55.8 102.2 all-gather.2
  169.8 39.0 reduce-scatter.1

commit v10 on v9

--- a/solution.py
+++ b/solution.py
@@ -58,7 +58,8 @@
     halves = lax.psum_scatter(partial_value, ("y", "c"), scatter_dimension=0, tiled=True)[0]
     mine = lax.dynamic_index_in_dim(halves, zh_index, 0, keepdims=False)
     other = lax.dynamic_index_in_dim(halves, 1 - zh_index, 0, keepdims=False)
-    summed = mine + lax.ppermute(other, "zh", [(0, 1), (1, 0)])
+    both_halves = lax.all_gather(other, "zh", axis=0, tiled=False)
+    summed = mine + lax.dynamic_index_in_dim(both_halves, 1 - zh_index, 0, keepdims=False)
     member = jnp.any(blocks_of[None, :] == own_blocks[:, None], axis=1)
     row_mask = jnp.repeat(member, BS)
     results = [jnp.where(row_mask[:, None], -summed, jnp.zeros_like(summed))]

time: 253 us -> 251 us (level)
  blocking collectives: 43.6 us -> 76.2 us
  waiting for transfers between devices: 160 us -> 138 us
  starting transfers between devices: 11.9 us -> 0.04 us
    all_gather x0 -> x1, blocking collectives: none -> 32.5 us  [body(): both_halves = lax.all_gather(other, 'zh', axis=0, tiled=False)]
    ppermute x1 -> x0, waiting for transfers between devices: 21.6 us -> none  [body(): summed = mine + lax.ppermute(other, 'zh', [(0, 1), (1, 0)])]
    ppermute x1 -> x0, starting transfers between devices: 11.8 us -> none  [body(): summed = mine + lax.ppermute(other, 'zh', [(0, 1), (1, 0)])]
  transfers between devices with their start and end apart: 3 -> 2, of which waited for: 3 -> 2; matrix products, arithmetic and copies ran while one was open for 1% -> 1% of each run, Pallas kernels for 0% -> 0%
where the time goes in v10:
time: 251 us
  waiting for transfers between devices  138 us (55%)
  blocking collectives  76.2 us (30%)
  between operations  13.5 us (5%)
  local copies, waits for them, and re-layouts  11.5 us (5%)
  matrix products  7.36 us (3%)
  other arithmetic  4.75 us (2%)
    all_gather x1, waiting for transfers between devices, body(): lax.all_gather(lax.all_gather(picked, 'x', axis=1, tiled=True), 'zl', axi...  99.3 us
    reduce_scatter x1, waiting for transfers between devices, body(): lax.psum_scatter(partial_value, ('y', 'c'), scatter_dimension=0, tiled=True)  38.4 us
    all_gather x1, blocking collectives, body(): both_halves = lax.all_gather(other, 'zh', axis=0, tiled=False)  32.5 us
    all_gather x1, blocking collectives, body(): gathered = lax.all_gather(dense, ('y', 'c'), axis=0, tiled=True)  16.9 us
    all_gather x1, blocking collectives, body(): both = lax.all_gather(pick(partner_col), 'zh', axis=0, tiled=False)  14.6 us
    all_gather x1, blocking collectives, body(): lax.all_gather(picked, 'x', axis=1, tiled=True)  12.1 us
    dot_general x1, matrix products, body(): jnp.einsum('mk,kyzcn->yczmn', anc_kept, rhs, preferred_element_type=jnp.f...  6.3 us
    transpose x1, local copies, waits for them, and re-layouts, body(): jnp.einsum('mk,kyzcn->yczmn', anc_kept, rhs, preferred_element_type=jnp.f...  5.22 us
  transfers between devices with their start and end apart: 2, of which 2 were waited for; matrix products, arithmetic and copies ran while one was open for 1% of the time, Pallas kernels for 0%

profile of v10, /device:TPU:25, one launch (start us, length us, event | category | flops | bytes accessed | tf_op | source)
XLA Modules:
  0.0 251.1 jit_solution(5774521085116143782)
XLA Ops:
  6.5 0.0 copy-start
  6.5 0.0 all-gather.4.cloned.1.call-start
  6.5 0.5 broadcast.216
  7.1 1.3 subtract_bitcast_fusion
  8.4 0.1 reshape_squeeze.6
  8.5 0.1 reshape.222
  8.6 1.1 copy.39
  9.6 0.1 reshape_squeeze.7
  9.8 16.9 %all_gather.19 = bf16[3072,128]{1,0:T(8,128)(2,1)S(1)} all-gather(bf16[384,128]{1,0:T(8,128)(2,1)S(1)} %reshape_squeeze.7), channel_id=1, replica_groups=mesh['zl'=8,'x'=4,'y'=4,'zh'=2,'c'=2] {'y','c'}, dimensions={0}, use_global_device_ids=true | all-gather | bytes 884736 | tf_op jit(solution)/shard_map/all_gather | solution.py:24
  26.7 0.8 convert_reduce_fusion
  27.6 0.5 convolution_convert_fusion
  28.1 14.6 %all-gather = bf16[14,64,128]{2,1,0:T(8,128)(2,1)S(1)} all-gather(bf16[7,64,128]{2,1,0:T(8,128)(2,1)S(1)} %copy.42), channel_id=2, replica_groups=mesh['zl'=8,'x'=4,'y'=4,'zh'=2,'c'=2] {'zh'}, dimensions={0}, use_global_device_ids=true | all-gather | bytes 344064 | tf_op jit(solution)/shard_map/all_gather | solution.py:42
  42.7 0.5 fusion
  43.3 0.1 reshape.224
  43.4 0.1 copy.45
  43.6 12.1 %all_gather.22 = bf16[896,256]{0,1:T(8,128)(2,1)} all-gather(bf16[896,64]{0,1:T(8,128)(2,1)S(1)} %copy.45), channel_id=1, replica_groups=mesh['zl'=8,'x'=4,'y'=4,'zh'=2,'c'=2] {'x'}, dimensions={1}, use_global_device_ids=true | all-gather | bytes 573440 | tf_op jit(solution)/shard_map/all_gather | solution.py:52
  55.7 0.0 all-gather.4.cloned.1.call-update
  55.7 0.0 reduce-scatter.2.cloned.1.call-start
  55.8 0.1 fusion.9
  55.9 0.2 reduce-window.8
  56.1 0.0 copy-done
  56.1 0.5 copy.46
  56.6 0.7 copy.47
  57.3 0.1 select_reduce_fusion
  57.4 0.7 gather_fusion
  58.2 0.2 select_bitcast_fusion
  58.3 0.5 copy.48
  58.9 99.3 %all-gather.4.cloned.1.call-done = bf16[896,2048]{0,1:T(8,128)(2,1)} async-done(((bf16[896,256]{0,1:T(8,128)(2,1)}), bf16[896,2048]{0,1:T(8,128)(2,1)}) %all-gather.4.cloned.1.call-update) | async-done | bytes 3670032 | tf_op jit(solution)/shard_map/all_gather | solution.py:52
  158.1 6.3 %convolution_bitcast_fusion = f32[4,2,2,512,128]{3,4,1,2,0:T(8,128)} fusion(bf16[896,4,2,2,128]{0,4,3,2,1:T(8,128)(2,1)} %bitcast.47, bf16[512,896,1,1,1]{0,1,4,3,2:T(8,128)(2,1)S(1)} %bitcast.43), kind=kOutput, calls=%fused_computation.1 | convolution fusion | flops 1879048192 | bytes 8781824 | tf_op jit(solution)/shard_map/mk,kyzcn->yczmn/dot_general | solution.py:56
  164.4 5.2 %copy.50 = f32[4,2,2,512,128]{4,3,2,1,0:T(8,128)} copy(f32[4,2,2,512,128]{3,4,1,2,0:T(8,128)} %convolution_bitcast_fusion) | data formatting | bytes 8388608 | tf_op jit(solution)/shard_map/mk,kyzcn->yczmn/transpose | solution.py:56
  169.6 0.0 copy-start.1
  169.6 0.0 reduce-scatter.2.cloned.1.call-update
  169.7 0.6 copy-done.1
  170.3 0.2 compare_reduce_fusion
  170.5 0.1 broadcast_bitcast_fusion
  170.6 38.4 %reduce-scatter.2.cloned.1.call-done = f32[1,2,512,128]{3,2,1,0:T(8,128)} async-done(((f32[8,2,512,128]{3,2,1,0:T(8,128)}), f32[1,2,512,128]{3,2,1,0:T(8,128)}) %reduce-scatter.2.cloned.1.call-update) | async-done | bytes 524304 | tf_op jit(solution)/shard_map/reduce_scatter | solution.py:58
  209.0 1.0 constant_dynamic-slice_fusion
  209.9 32.5 %all-gather.1 = f32[2,1,512,128]{3,2,1,0:T(8,128)S(1)} all-gather(f32[1,1,512,128]{3,2,1,0:T(8,128)S(1)} %constant_dynamic-slice_fusion), channel_id=3, replica_groups=mesh['zl'=8,'x'=4,'y'=4,'zh'=2,'c'=2] {'zh'}, dimensions={0}, use_global_device_ids=true | all-gather | bytes 786432 | tf_op jit(solution)/shard_map/all_gather | solution.py:61
  242.5 1.8 bitcast_select_fusion
  (12 shorter events, 0.1 us)
Async XLA Ops:
  6.5 49.5 %copy-start = (bf16[512,1024]{1,0:T(8,128)(2,1)S(1)}, bf16[512,1024]{1,0:T(8,128)(2,1)}, u32[]{:S(2)}) copy-start(bf16[512,1024]{1,0:T(8,128)(2,1)} %param.3) | copy-start | bytes 3145732
  6.5 151.6 %all-gather.4.cloned.1.call-start = ((), (), s32[]{:S(2)}) async-start(), calls=%async_computation.1 | async-start | bytes 4128768 | tf_op jit(solution)/shard_map/all_gather | solution.py:52
  55.7 153.3 %reduce-scatter.2.cloned.1.call-start = ((), (), s32[]{:S(2)}) async-start(), calls=%async_computation.2 | async-start | bytes 4718592 | tf_op jit(solution)/shard_map/reduce_scatter | solution.py:58
  169.6 0.7 copy-start.1
Sparse Core Ops, SparseCore 0:
  55.8 102.2 all-gather.3
  169.8 39.1 reduce-scatter.1

commit v11 on v10

--- a/solution.py
+++ b/solution.py
@@ -41,7 +41,7 @@
 
     both = lax.all_gather(pick(partner_col), "zh", axis=0, tiled=False)
     from_partner = lax.dynamic_index_in_dim(both, 1 - zh_index, 0, keepdims=False)
-    picked = (pick(col_index) + from_partner).reshape(CAP * BS, local_width)
+    picked = pick(col_index) + from_partner
     local_block = blocks_of - col_index * group_blocks
     hits = local_block[None, :] == block_ids[:, None]
     present = jnp.any(hits, axis=1)
@@ -49,7 +49,10 @@
     slot_of = present[None, :] & (rank[None, :] == slot_ids[:, None])
     slot_block = jnp.sum(jnp.where(slot_of, block_ids[None, :], 0), axis=1)
     anc_kept = jnp.take(anc_inv.reshape(local_rows, group_blocks, BS), slot_block, axis=1).reshape(local_rows, CAP * BS)
-    expanded = lax.all_gather(lax.all_gather(picked, "x", axis=1, tiled=True), "zl", axis=1, tiled=True)
+    n_x = lax.axis_size("x")
+    over_x = lax.all_gather(picked, "x", axis=0).reshape(n_x, CAP * BS, local_width)
+    over_x = over_x.transpose(1, 0, 2).reshape(CAP * BS, n_x * local_width)
+    expanded = lax.all_gather(over_x, "zl", axis=1, tiled=True)
     width = expanded.shape[1]
     chunk = width // (n_y * n_zh * n_c)
     rhs = expanded.reshape(-1, n_y, n_zh, n_c, chunk)

time: 251 us -> 252 us (level)
  no operation moved by 1% of the time
where the time goes in v11:
time: 252 us
  waiting for transfers between devices  138 us (55%)
  blocking collectives  75.6 us (30%)
  between operations  13.5 us (5%)
  local copies, waits for them, and re-layouts  12.7 us (5%)
  matrix products  7.36 us (3%)
  other arithmetic  4.75 us (2%)
    all_gather x1, waiting for transfers between devices, body(): expanded = lax.all_gather(over_x, 'zl', axis=1, tiled=True)  99.2 us
    reduce_scatter x1, waiting for transfers between devices, body(): lax.psum_scatter(partial_value, ('y', 'c'), scatter_dimension=0, tiled=True)  38.4 us
    all_gather x1, blocking collectives, body(): both_halves = lax.all_gather(other, 'zh', axis=0, tiled=False)  32.5 us
    all_gather x1, blocking collectives, body(): gathered = lax.all_gather(dense, ('y', 'c'), axis=0, tiled=True)  17.1 us
    all_gather x1, blocking collectives, body(): both = lax.all_gather(pick(partner_col), 'zh', axis=0, tiled=False)  14.6 us
    all_gather x1, blocking collectives, body(): lax.all_gather(picked, 'x', axis=0).reshape(n_x, CAP * BS, local_width)  11.4 us
    dot_general x1, matrix products, body(): jnp.einsum('mk,kyzcn->yczmn', anc_kept, rhs, preferred_element_type=jnp.f...  6.3 us
    transpose x1, local copies, waits for them, and re-layouts, body(): jnp.einsum('mk,kyzcn->yczmn', anc_kept, rhs, preferred_element_type=jnp.f...  5.22 us
  transfers between devices with their start and end apart: 2, of which 2 were waited for; matrix products, arithmetic and copies ran while one was open for 1% of the time, Pallas kernels for 0%

profile of v11, /device:TPU:25, one launch (start us, length us, event | category | flops | bytes accessed | tf_op | source)
XLA Modules:
  0.0 251.7 jit_solution(13265665426389206551)
XLA Ops:
  6.5 0.0 all-gather.5.cloned.1.call-start
  6.5 0.5 broadcast.216
  7.0 1.3 subtract_bitcast_fusion
  8.4 0.1 reshape_squeeze.6
  8.5 0.1 reshape.225
  8.6 1.1 copy.38
  9.6 0.1 reshape_squeeze.7
  9.8 0.0 copy-start
  9.8 17.1 %all_gather.22 = bf16[3072,128]{1,0:T(8,128)(2,1)S(1)} all-gather(bf16[384,128]{1,0:T(8,128)(2,1)S(1)} %reshape_squeeze.7), channel_id=1, replica_groups=mesh['zl'=8,'x'=4,'y'=4,'zh'=2,'c'=2] {'y','c'}, dimensions={0}, use_global_device_ids=true | all-gather | bytes 884736 | tf_op jit(solution)/shard_map/all_gather | solution.py:24
  26.9 0.8 convert_reduce_fusion
  27.7 0.5 convolution_convert_fusion
  28.3 14.6 %all-gather = bf16[14,64,128]{2,1,0:T(8,128)(2,1)S(1)} all-gather(bf16[7,64,128]{2,1,0:T(8,128)(2,1)S(1)} %copy.41), channel_id=2, replica_groups=mesh['zl'=8,'x'=4,'y'=4,'zh'=2,'c'=2] {'zh'}, dimensions={0}, use_global_device_ids=true | all-gather | bytes 344064 | tf_op jit(solution)/shard_map/all_gather | solution.py:42
  42.9 0.5 fusion
  43.4 11.4 %all-gather.1 = bf16[28,64,128]{2,1,0:T(8,128)(2,1)S(1)} all-gather(bf16[7,64,128]{2,1,0:T(8,128)(2,1)S(1)} %copy.43), channel_id=3, replica_groups=mesh['zl'=8,'x'=4,'y'=4,'zh'=2,'c'=2] {'x'}, dimensions={0}, use_global_device_ids=true | all-gather | bytes 573440 | tf_op jit(solution)/shard_map/all_gather | solution.py:53
  54.9 0.4 reshape.227
  55.3 1.1 copy.44
  56.4 0.0 all-gather.5.cloned.1.call-update
  56.4 0.0 reduce-scatter.2.cloned.1.call-start
  56.4 0.1 fusion.9
  56.6 0.2 reduce-window.8
  56.7 0.0 copy-done
  56.7 0.5 copy.45
  57.3 0.7 copy.46
  58.0 0.1 select_reduce_fusion
  58.1 0.7 gather_fusion
  58.8 0.2 select_bitcast_fusion
  59.0 0.5 copy.47
  59.5 99.2 %all-gather.5.cloned.1.call-done = bf16[896,2048]{0,1:T(8,128)(2,1)} async-done(((bf16[896,256]{0,1:T(8,128)(2,1)}), bf16[896,2048]{0,1:T(8,128)(2,1)}) %all-gather.5.cloned.1.call-update) | async-done | bytes 3670032 | tf_op jit(solution)/shard_map/all_gather | solution.py:55
  158.7 6.3 %convolution_bitcast_fusion = f32[4,2,2,512,128]{3,4,1,2,0:T(8,128)} fusion(bf16[896,4,2,2,128]{0,4,3,2,1:T(8,128)(2,1)} %bitcast.51, bf16[512,896,1,1,1]{0,1,4,3,2:T(8,128)(2,1)S(1)} %bitcast.47), kind=kOutput, calls=%fused_computation.1 | convolution fusion | flops 1879048192 | bytes 8781824 | tf_op jit(solution)/shard_map/mk,kyzcn->yczmn/dot_general | solution.py:59
  165.0 5.2 %copy.49 = f32[4,2,2,512,128]{4,3,2,1,0:T(8,128)} copy(f32[4,2,2,512,128]{3,4,1,2,0:T(8,128)} %convolution_bitcast_fusion) | data formatting | bytes 8388608 | tf_op jit(solution)/shard_map/mk,kyzcn->yczmn/transpose | solution.py:59
  170.3 0.0 copy-start.1
  170.3 0.0 reduce-scatter.2.cloned.1.call-update
  170.3 0.6 copy-done.1
  170.9 0.2 compare_reduce_fusion
  171.1 0.1 broadcast_bitcast_fusion
  171.2 38.4 %reduce-scatter.2.cloned.1.call-done = f32[1,2,512,128]{3,2,1,0:T(8,128)} async-done(((f32[8,2,512,128]{3,2,1,0:T(8,128)}), f32[1,2,512,128]{3,2,1,0:T(8,128)}) %reduce-scatter.2.cloned.1.call-update) | async-done | bytes 524304 | tf_op jit(solution)/shard_map/reduce_scatter | solution.py:61
  209.6 1.0 constant_dynamic-slice_fusion
  210.6 32.5 %all-gather.2 = f32[2,1,512,128]{3,2,1,0:T(8,128)S(1)} all-gather(f32[1,1,512,128]{3,2,1,0:T(8,128)S(1)} %constant_dynamic-slice_fusion), channel_id=4, replica_groups=mesh['zl'=8,'x'=4,'y'=4,'zh'=2,'c'=2] {'zh'}, dimensions={0}, use_global_device_ids=true | all-gather | bytes 786432 | tf_op jit(solution)/shard_map/all_gather | solution.py:64
  243.1 1.8 bitcast_select_fusion
  (12 shorter events, 0.1 us)
Async XLA Ops:
  6.5 152.2 %all-gather.5.cloned.1.call-start = ((), (), s32[]{:S(2)}) async-start(), calls=%async_computation.1 | async-start | bytes 4128768 | tf_op jit(solution)/shard_map/all_gather | solution.py:55
  9.8 47.0 %copy-start = (bf16[512,1024]{1,0:T(8,128)(2,1)S(1)}, bf16[512,1024]{1,0:T(8,128)(2,1)}, u32[]{:S(2)}) copy-start(bf16[512,1024]{1,0:T(8,128)(2,1)} %param.3) | copy-start | bytes 3145732
  56.4 153.2 %reduce-scatter.2.cloned.1.call-start = ((), (), s32[]{:S(2)}) async-start(), calls=%async_computation.2 | async-start | bytes 4718592 | tf_op jit(solution)/shard_map/reduce_scatter | solution.py:61
  170.3 0.7 copy-start.1
Sparse Core Ops, SparseCore 0:
  56.5 102.1 all-gather.4
  170.4 39.1 reduce-scatter.1
